TPU v7x, 256 devices: a whole 4x4x8 slice. The times are simulated.
256 devices in a mesh: kv: 8 (over z), blk: 32 (over y, x, core).
Axes of the slice: x: 4, y: 4, z: 8, core: 2. Of those that a mesh axis runs over, the one named last changes fastest.
Arguments:
- embeds: bfloat16 [1, 256, 3072], P(None, None, 'blk'), may hold values from -40 to 40
- attn_norm: float32 [3072], P('blk'), may hold values from 0.25 to 1.75
- query_key_value_weight: bfloat16 [3072, 5120], P('blk', 'kv'), may hold values from -0.109375 to 0.109375
- w_out: bfloat16 [3072, 3072], P('kv', 'blk'), may hold values from -0.109375 to 0.109375
- mlp_norm: float32 [3072], P('blk'), may hold values from 0.25 to 1.75
- w_gate: bfloat16 [3072, 8192], P('blk', 'kv'), may hold values from -0.109375 to 0.109375
- w_up: bfloat16 [3072, 8192], P('blk', 'kv'), may hold values from -0.109375 to 0.109375
- w_down: bfloat16 [8192, 3072], P('kv', 'blk'), may hold values from -0.0625 to 0.0625
- prompt_key_slots: bfloat16 [256, 8, 128, 128], P('blk', 'kv'), may hold values from -210 to 210
- prompt_value_slots: bfloat16 [256, 8, 128, 128], P('blk', 'kv'), may hold values from -6 to 6
- generated_keys: bfloat16 [256, 8, 127, 128], P('blk', 'kv'), may hold values from -10 to 10
- generated_values: bfloat16 [256, 8, 127, 128], P('blk', 'kv'), may hold values from -6 to 6
- parents: int32 [1, 256], P(None, 'blk'), may hold values from 0 to 7
- prompt_length: int32 [32], replicated, may hold values from 1024 to 8192
- tenant_bounds: int32 [5], replicated, may hold values from 0 to 32, as said below
- slot_table: int32 [256], P('blk'), may hold values from 0 to 256, as said below
Outputs:
- hidden_out: float32 [1, 256, 3072], P(None, None, 'blk')
- keys_out: bfloat16 [256, 8, 128, 128], P('blk', 'kv')
- values_out: bfloat16 [256, 8, 128, 128], P('blk', 'kv')
Inputs may be any that keep to these rules, and one draw needn't show every extreme that they name: parents[s, b] is the beam, among the 8 beams of b's request, whose cache beam b continues at step s. tenant_bounds[0] = 0 and tenant_bounds[4] = 32, strictly rising. `slot_table`: with L_t the largest prompt_length of tenant t's requests, every block j below ceil(L_t / 128) of every tenant t stands in exactly one slot as t * 64 + j, no other block stands anywhere, and 256 marks an empty slot.
All inputs are finite; a program needn't handle non-finite values.
Results may differ from a plain program's by a relative error of at most 0.012.
The roundings to bfloat16 on the way count: a program that leaves them out, or rounds other values in their place, can miss the bound.
Values may be sent and summed in bfloat16 or wider, within the bound.
No kernel may reach another device: no remote copies, remote signals or barrier semaphores. Data moves between devices by JAX's collectives and lax.ppermute only.
A program may use at most 64 MiB of HBM per device.

v0:
```python
import math

import jax
import jax.numpy as jnp
from jax import lax
from jax.sharding import PartitionSpec as P

MODEL_WIDTH = 3072
QUERY_HEADS = 24
KEY_VALUE_HEADS = 8
HEAD_WIDTH = 128
REQUEST_BEAMS = 8
TENANT_COUNT = 4
BLOCK_POSITIONS = 128
PROMPT_BLOCKS = 64
EARLIER_TOKENS = 127
DECODE_STEPS = 1


masked_score = -1e30


def merged(part, axis, combine):
    gathered = jax.tree.map(lambda a: lax.all_gather(a, axis), part)

    def take(source):
        return jax.tree.map(lambda a: lax.dynamic_index_in_dim(a, source, 0, False), gathered)

    return lax.fori_loop(
        1, lax.axis_size(axis), lambda source, state: combine(state, take(source)), take(0)
    )


def rotate(values, angles):
    half = values.shape[-1] // 2
    first = values[..., :half]
    second = values[..., half:]
    cosine = jnp.cos(angles)
    sine = jnp.sin(angles)
    return jnp.concatenate(
        [first * cosine - second * sine, second * cosine + first * sine], axis=-1
    )


def angles_for(positions, head_size):
    half = head_size // 2
    freq = jnp.exp(jnp.arange(half, dtype=jnp.float32) * (-math.log(500000.0) / half))
    return positions.astype(jnp.float32)[:, None] * freq[None, :]


def combine_parts(first, second):
    top_first, mass_first, sum_first = first
    top_second, mass_second, sum_second = second
    larger = jnp.maximum(top_first, top_second)
    factor_first = jnp.exp(top_first - larger)
    factor_second = jnp.exp(top_second - larger)
    return (
        larger,
        mass_first * factor_first + mass_second * factor_second,
        sum_first * factor_first[..., None] + sum_second * factor_second[..., None],
    )


def across_heads(partial_value):
    return lax.psum(partial_value, "kv")


def body(
    embeds,
    attn_norm,
    query_key_value_weight,
    w_out,
    mlp_norm,
    w_gate,
    w_up,
    w_down,
    prompt_key_slots,
    prompt_value_slots,
    generated_keys,
    generated_values,
    parents,
    prompt_length,
    tenant_bounds,
    slot_table,
):
    blocks = lax.axis_size("blk")
    my_index = lax.axis_index("blk")
    all_rows = embeds.shape[1]
    own_rows = all_rows // blocks
    heads_kv = prompt_key_slots.shape[1]
    slots_here = prompt_key_slots.shape[0]
    keys_here = slots_here * BLOCK_POSITIONS
    group_queries = QUERY_HEADS // KEY_VALUE_HEADS
    col_width = group_queries + 2
    score_scale = 1.0 / math.sqrt(HEAD_WIDTH)
    unit_count = w_gate.shape[1]
    beam_req = jnp.arange(all_rows, dtype=jnp.int32) // REQUEST_BEAMS
    tenant_beam = jnp.sum(
        (beam_req[:, None] >= tenant_bounds[None, 1:TENANT_COUNT]).astype(jnp.int32), axis=1
    )
    length_beam = jnp.repeat(prompt_length, REQUEST_BEAMS)
    slot_tenant = jnp.repeat(slot_table // PROMPT_BLOCKS, BLOCK_POSITIONS)
    slot_pos = jnp.repeat(slot_table % PROMPT_BLOCKS * BLOCK_POSITIONS, BLOCK_POSITIONS) + jnp.tile(
        jnp.arange(BLOCK_POSITIONS, dtype=jnp.int32), slots_here
    )
    visible = (tenant_beam[:, None] == slot_tenant[None, :]) & (
        slot_pos[None, :] < length_beam[:, None]
    )
    prompt_mask = visible[None, :, None, :]
    keys_flat = prompt_key_slots.transpose(1, 0, 2, 3).reshape(heads_kv, keys_here, HEAD_WIDTH)
    values_flat = prompt_value_slots.transpose(1, 0, 2, 3).reshape(heads_kv, keys_here, HEAD_WIDTH)
    local_beam = jnp.arange(own_rows, dtype=jnp.int32)
    base_rows = local_beam // REQUEST_BEAMS * REQUEST_BEAMS
    trailing_zeros = jnp.zeros((own_rows, heads_kv, DECODE_STEPS, HEAD_WIDTH), jnp.bfloat16)
    cached_key_rows = jnp.concatenate([generated_keys, trailing_zeros], axis=2)
    cached_value_rows = jnp.concatenate([generated_values, trailing_zeros], axis=2)
    gen_pos = jnp.arange(EARLIER_TOKENS + DECODE_STEPS, dtype=jnp.int32)
    w_both = jnp.concatenate([w_gate, w_up], axis=1)
    residual = embeds[0].astype(jnp.float32)
    squares = jnp.sum(residual * residual, axis=1)
    normed = (residual * attn_norm).astype(jnp.bfloat16)
    partial_value = jnp.dot(normed, query_key_value_weight, preferred_element_type=jnp.float32)
    total = lax.psum(squares, "blk")
    projected_rows = lax.psum(partial_value, "blk")
    inverse = lax.rsqrt(total / MODEL_WIDTH + 1e-05)
    projected_rows = (projected_rows * inverse[:, None]).reshape(
        all_rows, heads_kv, col_width, HEAD_WIDTH
    )
    angle_all = angles_for(length_beam + EARLIER_TOKENS + 0, HEAD_WIDTH)
    query_rows = rotate(projected_rows[:, :, :group_queries], angle_all[:, None, None, :]).astype(
        jnp.bfloat16
    )
    own_proj = lax.dynamic_slice_in_dim(projected_rows, my_index * own_rows, own_rows, 0)
    own_angle = lax.dynamic_slice_in_dim(angle_all, my_index * own_rows, own_rows, 0)
    new_key = rotate(own_proj[:, :, group_queries], own_angle[:, None, :]).astype(jnp.bfloat16)
    new_value = own_proj[:, :, group_queries + 1].astype(jnp.bfloat16)
    parent_rows = base_rows + parents[0]
    cached_key_rows = (
        jnp.take(cached_key_rows, parent_rows, axis=0).at[:, :, EARLIER_TOKENS].set(new_key)
    )
    cached_value_rows = (
        jnp.take(cached_value_rows, parent_rows, axis=0).at[:, :, EARLIER_TOKENS].set(new_value)
    )
    grouped = query_rows.transpose(1, 0, 2, 3).reshape(
        heads_kv, all_rows * group_queries, HEAD_WIDTH
    )
    scores = jnp.einsum("kqd,knd->kqn", grouped, keys_flat, preferred_element_type=jnp.float32)
    scores = scores.reshape(heads_kv, all_rows, group_queries, keys_here) * score_scale
    top_score = jnp.max(jnp.where(prompt_mask, scores, masked_score), axis=3)
    weights = jnp.where(prompt_mask, jnp.exp(scores - top_score[..., None]), 0.0)
    total_mass = jnp.sum(weights, axis=3)
    flat_weights = weights.reshape(heads_kv, all_rows * group_queries, keys_here).astype(
        jnp.bfloat16
    )
    summed = jnp.einsum(
        "kqn,knd->kqd", flat_weights, values_flat, preferred_element_type=jnp.float32
    )
    summed = summed.reshape(heads_kv, all_rows, group_queries, HEAD_WIDTH)
    all_top, all_mass, all_sum = merged((top_score, total_mass, summed), "blk", combine_parts)
    prompt_top = lax.dynamic_slice_in_dim(all_top, my_index * own_rows, own_rows, 1)
    prompt_mass = lax.dynamic_slice_in_dim(all_mass, my_index * own_rows, own_rows, 1)
    prompt_sum = lax.dynamic_slice_in_dim(all_sum, my_index * own_rows, own_rows, 1)
    own_queries = lax.dynamic_slice_in_dim(query_rows, my_index * own_rows, own_rows, 0)
    gen_scores = (
        jnp.einsum(
            "bkgd,bknd->kbgn", own_queries, cached_key_rows, preferred_element_type=jnp.float32
        )
        * score_scale
    )
    live = (gen_pos <= EARLIER_TOKENS)[None, None, None, :]
    gen_top = jnp.max(jnp.where(live, gen_scores, masked_score), axis=3)
    best = jnp.maximum(prompt_top, gen_top)
    gen_weights = jnp.where(live, jnp.exp(gen_scores - best[..., None]), 0.0)
    shift = jnp.exp(prompt_top - best)
    full_mass = prompt_mass * shift + jnp.sum(gen_weights, axis=3)
    gen_sum = jnp.einsum(
        "kbgn,bknd->kbgd",
        gen_weights.astype(jnp.bfloat16),
        cached_value_rows,
        preferred_element_type=jnp.float32,
    )
    attended_output = (prompt_sum * shift[..., None] + gen_sum) / full_mass[..., None]
    heads_out = (
        attended_output.transpose(1, 0, 2, 3)
        .reshape(own_rows, heads_kv * group_queries * HEAD_WIDTH)
        .astype(jnp.bfloat16)
    )
    head_part = jnp.dot(
        lax.all_gather(heads_out, "blk", axis=0, tiled=True),
        w_out,
        preferred_element_type=jnp.float32,
    )
    after_attn = residual + across_heads(head_part)
    total2 = lax.psum(jnp.sum(after_attn * after_attn, axis=1), "blk")
    inverse2 = lax.rsqrt(total2 / MODEL_WIDTH + 1e-05)
    normed2 = (after_attn * mlp_norm).astype(jnp.bfloat16)
    mixed = lax.psum_scatter(
        jnp.dot(normed2, w_both, preferred_element_type=jnp.float32),
        "blk",
        scatter_dimension=0,
        tiled=True,
    )
    own_inverse = lax.dynamic_slice_in_dim(inverse2, my_index * own_rows, own_rows, 0)
    gate = mixed[:, :unit_count] * own_inverse[:, None]
    upper = mixed[:, unit_count:] * own_inverse[:, None]
    hidden = (jax.nn.silu(gate) * upper).astype(jnp.bfloat16)
    ff_part = jnp.dot(
        lax.all_gather(hidden, "blk", axis=0, tiled=True),
        w_down,
        preferred_element_type=jnp.float32,
    )
    outputs = [after_attn + across_heads(ff_part)]
    return (jnp.stack(outputs), cached_key_rows, cached_value_rows)


def solution(mesh):
    in_specs = (
        P(None, None, "blk"),
        P("blk"),
        P("blk", "kv"),
        P("kv", "blk"),
        P("blk"),
        P("blk", "kv"),
        P("blk", "kv"),
        P("kv", "blk"),
        P("blk", "kv", None, None),
        P("blk", "kv", None, None),
        P("blk", "kv", None, None),
        P("blk", "kv", None, None),
        P(None, "blk"),
        P(),
        P(),
        P("blk"),
    )
    out_specs = (P(None, None, "blk"), P("blk", "kv", None, None), P("blk", "kv", None, None))
    return jax.shard_map(body, mesh=mesh, in_specs=in_specs, out_specs=out_specs, check_vma=False)
```

profile of v0, /device:TPU:2, one launch (start us, length us, event | category | flops | bytes accessed | tf_op | source)
XLA Modules:
  0.0 575.9 jit_solution(11077817776929856771)
XLA Ops:
  7.2 2.2 fusion.25
  11.0 62.3 %psum.36 = f32[256]{0:T(256)S(1)} all-reduce(f32[256]{0:T(256)S(1)} %fusion.24), channel_id=1, replica_groups=mesh['kv'=8,'blk'=32] {'blk'}, use_global_device_ids=true, to_apply=%region_3.4 | all-reduce | flops 256 | bytes 2048 | tf_op jit(solution)/shard_map/psum | solution.py:123
  77.1 49.7 %all-reduce.6.cloned.1.call-done = f32[256,640]{1,0:T(8,128)} async-done(((f32[256,640]{1,0:T(8,128)}), f32[256,640]{1,0:T(8,128)}) %all-reduce.6.cloned.1.call-update) | async-done | bytes 655376 | tf_op jit(solution)/shard_map/psum | solution.py:124
  129.4 1.8 select_reduce_fusion
  131.2 2.6 fusion.6
  134.9 1.7 copy.130
  137.4 2.2 gather_fusion
  139.6 1.7 pad_bitcast_fusion
  141.3 2.2 gather_fusion.1
  143.5 1.9 bitcast_select_fusion.1
  147.6 1.3 scatter.6
  151.1 23.0 %all-gather = f32[8192,3]{0,1:T(4,128)S(1)} all-gather(f32[256,3]{0,1:T(4,128)S(1)} %get-tuple-element.301), channel_id=2, replica_groups=mesh['kv'=8,'blk'=32] {'blk'}, dimensions={0}, use_global_device_ids=true | all-gather | bytes 101376 | tf_op jit(solution)/shard_map/all_gather | solution.py:24
  174.1 2.0 fusion.5
  176.1 24.7 %all-gather.1 = f32[8192,3]{0,1:T(4,128)S(1)} all-gather(f32[256,3]{0,1:T(4,128)S(1)} %fusion.5), channel_id=3, replica_groups=mesh['kv'=8,'blk'=32] {'blk'}, dimensions={0}, use_global_device_ids=true | all-gather | bytes 101376 | tf_op jit(solution)/shard_map/all_gather | solution.py:24
  200.9 1.4 scatter.9
  203.6 82.1 %while.21 = (s32[]{:T(128)}, f32[1,256,3]{1,0,2:T(1,128)S(1)}, f32[1,256,3]{1,0,2:T(1,128)S(1)}, f32[1,256,3,128]{3,2,1,0:T(4,128)S(1)}, f32[32,1,256,3]{2,0,3,1...) while((s32[]{:T(128)}, f32[1,256,3]{1,0,2:T(1,128)S(1)}, ...), condition=%wide.region_7.8_spmd, body=%wide.region_6.7_spmd.sunk | while | flops 299525 | bytes 2009231 | solution.py:29
  286.6 22.7 %all_gather.26 = bf16[256,384]{1,0:T(8,128)(2,1)S(1)} all-gather(bf16[8,384]{1,0:T(8,128)(2,1)S(1)} %bitcast.190), channel_id=1, replica_groups=mesh['kv'=8,'blk'=32] {'blk'}, dimensions={0}, use_global_device_ids=true | all-gather | bytes 202752 | tf_op jit(solution)/shard_map/all_gather | solution.py:189
  310.2 72.3 %all-reduce.8.cloned.1.call-done = f32[256,96]{0,1:T(8,128)} async-done(((f32[256,96]{0,1:T(8,128)}), f32[256,96]{0,1:T(8,128)}) %all-reduce.8.cloned.1.call-update) | async-done | bytes 98320 | tf_op jit(solution)/shard_map/psum | solution.py:65
  382.5 2.8 fusion.13
  385.4 57.6 %psum.38 = f32[256]{0:T(256)S(1)} all-reduce(f32[256]{0:T(256)S(1)} %multiply_reduce_fusion), channel_id=1, replica_groups=mesh['kv'=8,'blk'=32] {'blk'}, use_global_device_ids=true, to_apply=%region_13.15 | all-reduce | flops 256 | bytes 2048 | tf_op jit(solution)/shard_map/psum | solution.py:194
  443.2 27.7 %reduce-scatter.2.cloned.1.call-done = f32[8,2048]{1,0:T(8,128)} async-done(((f32[256,2048]{1,0:T(8,128)}), f32[8,2048]{1,0:T(8,128)}) %reduce-scatter.2.cloned.1.call-update) | async-done | bytes 65552 | tf_op jit(solution)/shard_map/reduce_scatter | solution.py:197
  471.7 23.1 %all_gather.27 = bf16[256,1024]{1,0:T(8,128)(2,1)S(1)} all-gather(bf16[8,1024]{1,0:T(8,128)(2,1)S(1)} %fusion.31), channel_id=1, replica_groups=mesh['kv'=8,'blk'=32] {'blk'}, dimensions={0}, use_global_device_ids=true | all-gather | bytes 540672 | tf_op jit(solution)/shard_map/all_gather | solution.py:208
  495.8 72.0 %all-reduce.10.cloned.1.call-done = f32[256,96]{0,1:T(8,128)} async-done(((f32[256,96]{0,1:T(8,128)}), f32[256,96]{0,1:T(8,128)}) %all-reduce.10.cloned.1.call-update) | async-done | bytes 98320 | tf_op jit(solution)/shard_map/psum | solution.py:65
  567.8 1.5 add_bitcast_fusion
  (253 shorter events, 99.9 us)
Async XLA Ops:
  7.2 121.5 %copy-start = (bf16[8,1,128,128]{3,2,1,0:T(8,128)(2,1)S(1)}, bf16[8,1,128,128]{3,2,1,0:T(8,128)(2,1)}, u32[]{:S(2)}) copy-start(bf16[8,1,128,128]{3,2,1,0:T(8,128)(2,1)} %param.32) | copy-start | bytes 786436
  7.2 119.6 %all-reduce.6.cloned.1.call-start = ((), (), s32[]{:S(2)}) async-start(), calls=%async_computation.1 | async-start | bytes 1310720 | tf_op jit(solution)/shard_map/psum | solution.py:124
  9.4 192.8 %all-gather.5.cloned.1.call-start = ((), (), s32[]{:S(2)}) async-start(), calls=%async_computation.5 | async-start | bytes 12976128 | tf_op jit(solution)/shard_map/all_gather | solution.py:24
  128.2 0.9 copy-start.1
  128.7 0.7 copy-start.2
  128.7 2.5 copy-start.3
  131.2 5.4 copy-start.12
  133.9 248.6 %all-reduce.8.cloned.1.call-start = ((), (), s32[]{:S(2)}) async-start(), calls=%async_computation.2 | async-start | bytes 196608 | tf_op jit(solution)/shard_map/psum | solution.py:65
  203.5 82.8 %copy-start.6 = (bf16[8,1,128,128]{3,2,0,1:T(8,128)(2,1)S(1)}, bf16[8,1,128,128]{3,2,0,1:T(8,128)(2,1)}, u32[]{:S(2)}) copy-start(bf16[8,1,128,128]{3,2,0,1:T(8,128)(2,1)} %scatter.9) | copy-start | bytes 786436
  203.5 105.7 %copy-start.10 = (bf16[384,96]{0,1:T(8,128)(2,1)S(1)}, bf16[384,96]{0,1:T(8,128)(2,1)}, u32[]{:S(2)}) copy-start(bf16[384,96]{0,1:T(8,128)(2,1)} %param.27) | copy-start | bytes 221188
  203.5 178.9 %copy-start.4 = (bf16[1,256,96]{1,2,0:T(8,128)(2,1)S(1)}, bf16[1,256,96]{1,2,0:T(8,128)(2,1)}, u32[]{:S(2)}) copy-start(bf16[1,256,96]{1,2,0:T(8,128)(2,1)} %param.24) | copy-start | bytes 147460
  203.6 178.9 %copy-start.7 = (bf16[96,1024]{1,0:T(8,128)(2,1)S(1)}, bf16[96,1024]{1,0:T(8,128)(2,1)}, u32[]{:S(2)}) copy-start(bf16[96,1024]{1,0:T(8,128)(2,1)} %param.30) | copy-start | bytes 589828
  203.6 178.9 %copy-start.8 = (bf16[96,1024]{1,0:T(8,128)(2,1)S(1)}, bf16[96,1024]{1,0:T(8,128)(2,1)}, u32[]{:S(2)}) copy-start(bf16[96,1024]{1,0:T(8,128)(2,1)} %param.29) | copy-start | bytes 589828
  203.6 178.9 %copy-start.11 = (f32[96]{0:T(128)S(1)}, f32[96]{0:T(128)}, u32[]{:S(2)}) copy-start(f32[96]{0:T(128)} %param.28) | copy-start | bytes 1156
  286.6 208.3 %copy-start.9 = (bf16[1024,96]{0,1:T(8,128)(2,1)S(1)}, bf16[1024,96]{0,1:T(8,128)(2,1)}, u32[]{:S(2)}) copy-start(bf16[1024,96]{0,1:T(8,128)(2,1)} %param.31) | copy-start | bytes 589828
  310.2 160.7 %reduce-scatter.2.cloned.1.call-start = ((), (), s32[]{:S(2)}) async-start(), calls=%async_computation.3 | async-start | bytes 2162688 | tf_op jit(solution)/shard_map/reduce_scatter | solution.py:197
  382.5 2.9 copy-start.5
  385.3 182.5 %all-reduce.10.cloned.1.call-start = ((), (), s32[]{:S(2)}) async-start(), calls=%async_computation.4 | async-start | bytes 196608 | tf_op jit(solution)/shard_map/psum | solution.py:65
Sparse Core Ops, SparseCore 0:
  11.2 115.4 all-reduce.5
  134.0 68.0 all-gather.4
  310.3 72.1 all-reduce.7
  386.6 84.1 reduce-scatter.1
  496.0 71.8 all-reduce.9
where the time goes:
time: 578 us; the launch traced here: 576 us
  waiting for transfers between devices  222 us (38%)
  blocking collectives  213 us (37%)
  local copies, waits for them, and re-layouts  58.7 us (10%)
  other arithmetic  53.6 us (9%)
  between operations  14.1 us (2%)
  matrix products  12.7 us (2%)
    psum x2, waiting for transfers between devices, across_heads(): return lax.psum(partial_value, 'kv')  144 us
    psum x1, blocking collectives, body(): total = lax.psum(squares, 'blk')  62.3 us
    psum x1, blocking collectives, body(): total2 = lax.psum(jnp.sum(after_attn * after_attn, axis=1), 'blk')  57.6 us
    psum x1, waiting for transfers between devices, body(): projected_rows = lax.psum(partial_value, 'blk')  49.7 us
    all_gather x2, blocking collectives, merged(): gathered = jax.tree.map(lambda a: lax.all_gather(a, axis), part)  47.8 us
    add x31, other arithmetic, combine_parts(): sum_first * factor_first[..., None] + sum_second * factor_second[..., None]  39.1 us
    dynamic_slice x33, local copies, waits for them, and re-layouts, take(): lax.dynamic_index_in_dim(a, source, 0, False)  32 us
    reduce_scatter x1, waiting for transfers between devices, body(): lax.psum_scatter(jnp.dot(normed2, w_both, preferred_element_type=jnp.floa...  27.7 us
  transfers between devices with their start and end apart: 5, of which 4 were waited for; matrix products, arithmetic and copies ran while one was open for 5% of the time, Pallas kernels for 0%

commit v1 on v0

--- a/solution.py
+++ b/solution.py
@@ -20,15 +20,24 @@
 masked_score = -1e30
 
 
-def merged(part, axis, combine):
-    gathered = jax.tree.map(lambda a: lax.all_gather(a, axis), part)
-
-    def take(source):
-        return jax.tree.map(lambda a: lax.dynamic_index_in_dim(a, source, 0, False), gathered)
-
-    return lax.fori_loop(
-        1, lax.axis_size(axis), lambda source, state: combine(state, take(source)), take(0)
-    )
+def exchange(value, axis, bit):
+    count = lax.axis_size(axis)
+    return lax.ppermute(value, axis, [(i, i ^ (1 << bit)) for i in range(count)])
+
+
+def butterfly_sum(value, axis):
+    count = lax.axis_size(axis)
+    if count & (count - 1):
+        return lax.psum(value, axis)
+    for bit in range(count.bit_length() - 1):
+        value = value + exchange(value, axis, bit)
+    return value
+
+
+def scatter_sum(value, axis):
+    count = lax.axis_size(axis)
+    pieces = value.reshape((count, value.shape[0] // count) + value.shape[1:])
+    return jnp.sum(lax.all_to_all(pieces, axis, 0, 0, tiled=False), axis=0)
 
 
 def rotate(values, angles):
@@ -48,21 +57,8 @@
     return positions.astype(jnp.float32)[:, None] * freq[None, :]
 
 
-def combine_parts(first, second):
-    top_first, mass_first, sum_first = first
-    top_second, mass_second, sum_second = second
-    larger = jnp.maximum(top_first, top_second)
-    factor_first = jnp.exp(top_first - larger)
-    factor_second = jnp.exp(top_second - larger)
-    return (
-        larger,
-        mass_first * factor_first + mass_second * factor_second,
-        sum_first * factor_first[..., None] + sum_second * factor_second[..., None],
-    )
-
-
 def across_heads(partial_value):
-    return lax.psum(partial_value, "kv")
+    return butterfly_sum(partial_value, "kv")
 
 
 def body(
@@ -120,18 +116,15 @@
     squares = jnp.sum(residual * residual, axis=1)
     normed = (residual * attn_norm).astype(jnp.bfloat16)
     partial_value = jnp.dot(normed, query_key_value_weight, preferred_element_type=jnp.float32)
-    total = lax.psum(squares, "blk")
-    projected_rows = lax.psum(partial_value, "blk")
-    inverse = lax.rsqrt(total / MODEL_WIDTH + 1e-05)
-    projected_rows = (projected_rows * inverse[:, None]).reshape(
-        all_rows, heads_kv, col_width, HEAD_WIDTH
-    )
-    angle_all = angles_for(length_beam + EARLIER_TOKENS + 0, HEAD_WIDTH)
-    query_rows = rotate(projected_rows[:, :, :group_queries], angle_all[:, None, None, :]).astype(
+    own_value = scatter_sum(jnp.concatenate([partial_value, squares[:, None]], axis=1), "blk")
+    inverse = lax.rsqrt(own_value[:, -1] / MODEL_WIDTH + 1e-05)
+    own_proj = (own_value[:, :-1] * inverse[:, None]).reshape(own_rows, heads_kv, col_width, HEAD_WIDTH)
+    own_length = lax.dynamic_slice_in_dim(length_beam, my_index * own_rows, own_rows, 0)
+    own_angle = angles_for(own_length + EARLIER_TOKENS + 0, HEAD_WIDTH)
+    own_queries = rotate(own_proj[:, :, :group_queries], own_angle[:, None, None, :]).astype(
         jnp.bfloat16
     )
-    own_proj = lax.dynamic_slice_in_dim(projected_rows, my_index * own_rows, own_rows, 0)
-    own_angle = lax.dynamic_slice_in_dim(angle_all, my_index * own_rows, own_rows, 0)
+    query_rows = lax.all_gather(own_queries, "blk", axis=0, tiled=True)
     new_key = rotate(own_proj[:, :, group_queries], own_angle[:, None, :]).astype(jnp.bfloat16)
     new_value = own_proj[:, :, group_queries + 1].astype(jnp.bfloat16)
     parent_rows = base_rows + parents[0]
@@ -156,11 +149,19 @@
         "kqn,knd->kqd", flat_weights, values_flat, preferred_element_type=jnp.float32
     )
     summed = summed.reshape(heads_kv, all_rows, group_queries, HEAD_WIDTH)
-    all_top, all_mass, all_sum = merged((top_score, total_mass, summed), "blk", combine_parts)
-    prompt_top = lax.dynamic_slice_in_dim(all_top, my_index * own_rows, own_rows, 1)
-    prompt_mass = lax.dynamic_slice_in_dim(all_mass, my_index * own_rows, own_rows, 1)
-    prompt_sum = lax.dynamic_slice_in_dim(all_sum, my_index * own_rows, own_rows, 1)
-    own_queries = lax.dynamic_slice_in_dim(query_rows, my_index * own_rows, own_rows, 0)
+    packed = jnp.concatenate([summed, top_score[..., None], total_mass[..., None]], axis=3)
+    packed = packed.transpose(1, 0, 2, 3).reshape(
+        blocks, own_rows, heads_kv, group_queries, HEAD_WIDTH + 2
+    )
+    parts = lax.all_to_all(packed, "blk", 0, 0, tiled=False)
+    part_top = parts[..., HEAD_WIDTH]
+    prompt_top = jnp.max(part_top, axis=0)
+    part_factor = jnp.exp(part_top - prompt_top[None])
+    prompt_mass = jnp.sum(parts[..., HEAD_WIDTH + 1] * part_factor, axis=0)
+    prompt_sum = jnp.sum(parts[..., :HEAD_WIDTH] * part_factor[..., None], axis=0)
+    prompt_top = prompt_top.transpose(1, 0, 2)
+    prompt_mass = prompt_mass.transpose(1, 0, 2)
+    prompt_sum = prompt_sum.transpose(1, 0, 2, 3)
     gen_scores = (
         jnp.einsum(
             "bkgd,bknd->kbgn", own_queries, cached_key_rows, preferred_element_type=jnp.float32
@@ -191,18 +192,18 @@
         preferred_element_type=jnp.float32,
     )
     after_attn = residual + across_heads(head_part)
-    total2 = lax.psum(jnp.sum(after_attn * after_attn, axis=1), "blk")
-    inverse2 = lax.rsqrt(total2 / MODEL_WIDTH + 1e-05)
+    squares2 = jnp.sum(after_attn * after_attn, axis=1)
     normed2 = (after_attn * mlp_norm).astype(jnp.bfloat16)
-    mixed = lax.psum_scatter(
-        jnp.dot(normed2, w_both, preferred_element_type=jnp.float32),
+    mixed = scatter_sum(
+        jnp.concatenate(
+            [jnp.dot(normed2, w_both, preferred_element_type=jnp.float32), squares2[:, None]],
+            axis=1,
+        ),
         "blk",
-        scatter_dimension=0,
-        tiled=True,
-    )
-    own_inverse = lax.dynamic_slice_in_dim(inverse2, my_index * own_rows, own_rows, 0)
+    )
+    own_inverse = lax.rsqrt(mixed[:, -1] / MODEL_WIDTH + 1e-05)
     gate = mixed[:, :unit_count] * own_inverse[:, None]
-    upper = mixed[:, unit_count:] * own_inverse[:, None]
+    upper = mixed[:, unit_count : 2 * unit_count] * own_inverse[:, None]
     hidden = (jax.nn.silu(gate) * upper).astype(jnp.bfloat16)
     ff_part = jnp.dot(
         lax.all_gather(hidden, "blk", axis=0, tiled=True),

time: 578 us -> 211 us (0.37)
  waiting for transfers between devices: 222 us -> 49.7 us
  blocking collectives: 213 us -> 104 us
  local copies, waits for them, and re-layouts: 58.7 us -> 5.57 us
  other arithmetic: 53.6 us -> 10.9 us
  starting transfers between devices: 0.21 us -> 32.7 us
  between operations: 14.1 us -> 1.09 us
  matrix products: 12.7 us -> 6.5 us
    psum x3 -> x0, waiting for transfers between devices: 194 us -> none  [the longest x2 144 us: across_heads(): return lax.psum(partial_value, 'kv')]
    psum x2 -> x0, blocking collectives: 120 us -> none  [the longest x1 62.3 us: body(): total = lax.psum(squares, 'blk')]
    add x62 -> x5, other arithmetic: 40.2 us -> 0.06 us  [the longest x4 0.05 us: butterfly_sum(): value = value + exchange(value, axis, bit)]
    all_to_all x0 -> x1, blocking collectives: none -> 34.6 us  [scatter_sum(): return jnp.sum(lax.all_to_all(pieces, axis, 0, 0, tiled=False), axis=0)]
    dynamic_slice x35 -> x0, local copies, waits for them, and re-layouts: 33.2 us -> none  [the longest x33 32 us: take(): lax.dynamic_index_in_dim(a, source, 0, False)]
    ppermute x0 -> x6, waiting for transfers between devices: none -> 27.9 us  [exchange(): return lax.ppermute(value, axis, [(i, i ^ 1 << bit) for i in range(count)])]
    reduce_scatter x1 -> x0, waiting for transfers between devices: 27.7 us -> none  [body(): lax.psum_scatter(jnp.dot(normed2, w_both, preferred_element_type=jnp.floa...]
    all_gather x2 -> x1, blocking collectives: 47.8 us -> 22.9 us  [body(): query_rows = lax.all_gather(own_queries, 'blk', axis=0, tiled=True)]
  transfers between devices with their start and end apart: 5 -> 8, of which waited for: 4 -> 8; matrix products, arithmetic and copies ran while one was open for 5% -> 2% of each run, Pallas kernels for 0% -> 0%
where the time goes in v1:
time: 211 us; the launch traced here: 210 us
  blocking collectives  104 us (49%)
  waiting for transfers between devices  49.7 us (24%)
  starting transfers between devices  32.7 us (15%)
  other arithmetic  10.9 us (5%)
  matrix products  6.5 us (3%)
  local copies, waits for them, and re-layouts  5.57 us (3%)
    all_to_all x1, blocking collectives, scatter_sum(): return jnp.sum(lax.all_to_all(pieces, axis, 0, 0, tiled=False), axis=0)  34.6 us
    ppermute x6, waiting for transfers between devices, exchange(): return lax.ppermute(value, axis, [(i, i ^ 1 << bit) for i in range(count)])  27.9 us
    all_gather x1, blocking collectives, body(): lax.all_gather(hidden, 'blk', axis=0, tiled=True)  23.3 us
    all_gather x1, blocking collectives, body(): lax.all_gather(heads_out, 'blk', axis=0, tiled=True)  23.1 us
    all_gather x1, blocking collectives, body(): query_rows = lax.all_gather(own_queries, 'blk', axis=0, tiled=True)  22.9 us
    ppermute x6, starting transfers between devices, exchange(): return lax.ppermute(value, axis, [(i, i ^ 1 << bit) for i in range(count)])  19.3 us
    all_to_all x1, waiting for transfers between devices, body(): parts = lax.all_to_all(packed, 'blk', 0, 0, tiled=False)  12.5 us
    all_to_all x1, waiting for transfers between devices, scatter_sum(): return jnp.sum(lax.all_to_all(pieces, axis, 0, 0, tiled=False), axis=0)  9.32 us
  transfers between devices with their start and end apart: 8, of which 8 were waited for; matrix products, arithmetic and copies ran while one was open for 2% of the time, Pallas kernels for 0%

profile of v1, /device:TPU:2, one launch (start us, length us, event | category | flops | bytes accessed | tf_op | source)
XLA Modules:
  0.0 210.3 jit_solution(3467085731439705462)
XLA Ops:
  2.7 1.1 fusion.21
  4.8 7.6 %all-to-all-start = ((f32[32,8,641]{2,1,0:T(8,128)}), f32[32,8,641]{2,1,0:T(8,128)S(1)}, u32[]{:S(2)}, u32[]{:S(2)}) async-start(f32[32,8,641]{2,1,0:T(8,128)} %pad_maximum_fusion.1), calls=%async_computation | async-start | bytes 1572864 | tf_op jit(solution)/shard_map/all_to_all | solution.py:40
  16.4 9.3 %all-to-all-done = f32[32,8,641]{2,1,0:T(8,128)S(1)} async-done(((f32[32,8,641]{2,1,0:T(8,128)}), f32[32,8,641]{2,1,0:T(8,128)S(1)}, u32[]{:S(2)}, u32[]{:S(2)}) %all-to-all-start) | async-done | bytes 656416 | tf_op jit(solution)/shard_map/all_to_all | solution.py:40
  26.2 22.9 %all_gather.9 = bf16[256,1,3,128]{3,0,2,1:T(8,128)(2,1)S(1)} all-gather(bf16[8,1,3,128]{3,0,2,1:T(8,128)(2,1)S(1)} %pad_maximum_fusion.2), channel_id=1, replica_groups=mesh['kv'=8,'blk'=32] {'blk'}, dimensions={0}, use_global_device_ids=true | all-gather | bytes 202752 | tf_op jit(solution)/shard_map/all_gather | solution.py:127
  49.0 1.8 select_reduce_fusion
  50.9 3.1 %fusion.2 = (bf16[32,8,3,1024]{3,1,0,2:T(8,128)(2,1)}, f32[256,3]{0,1:T(4,128)S(1)}) fusion(f32[256,3,1024]{2,0,1:T(8,128)S(1)} %get-tuple-element.71, f32[256,3]{0,1:T(4,128)S(1)} %get-tuple-element.70, pred[256,1024]{1,0:T(8,128)(4,1)} %compare_and_fusion), kind=kLoop, calls=%fused_computation.8 | loop fusion | flops 3931392 | bytes 4986880 | tf_op jit(solution)/shard_map/reshape.462
  55.4 2.0 fusion.5
  57.4 1.1 maximum_bitcast_fusion
  58.5 5.7 %all-to-all-start.1 = ((f32[32,8,1,3,130]{4,1,3,2,0:T(8,128)}), f32[32,8,1,3,130]{4,1,3,2,0:T(8,128)S(1)}, u32[]{:S(2)}, u32[]{:S(2)}) async-start(f32[32,8,1,3,130]{4,1,3,2,0:T(8,128)} %maximum_bitcast_fusion), calls=%async_computation.1 | async-start | bytes 1572864 | tf_op jit(solution)/shard_map/all_to_all | solution.py:156
  65.1 12.5 %all-to-all-done.1 = f32[32,8,1,3,130]{4,1,3,2,0:T(8,128)S(1)} async-done(((f32[32,8,1,3,130]{4,1,3,2,0:T(8,128)}), f32[32,8,1,3,130]{4,1,3,2,0:T(8,128)S(1)}, u32[]{:S(2)}, u32[]{:S(2)}) %all-to-all-start.1) | async-done | bytes 399392 | tf_op jit(solution)/shard_map/all_to_all | solution.py:156
  79.5 23.1 %all_gather.10 = bf16[256,384]{1,0:T(8,128)(2,1)S(1)} all-gather(bf16[8,384]{1,0:T(8,128)(2,1)S(1)} %bitcast.108), channel_id=1, replica_groups=mesh['kv'=8,'blk'=32] {'blk'}, dimensions={0}, use_global_device_ids=true | all-gather | bytes 202752 | tf_op jit(solution)/shard_map/all_gather | solution.py:190
  102.8 2.0 collective-permute-start
  104.8 3.3 %collective-permute-done = f32[256,96]{0,1:T(8,128)S(1)} collective-permute-done((f32[256,96]{0,1:T(8,128)S(1)}, f32[256,96]{0,1:T(8,128)S(1)}, u32[]{:S(2)}, u32[]{:S(2)}) %collective-permute-start) | collective-permute-done | bytes 98336 | tf_op jit(solution)/shard_map/ppermute | solution.py:25
  108.1 3.4 %collective-permute-start.1 = (f32[256,96]{0,1:T(8,128)S(1)}, f32[256,96]{0,1:T(8,128)S(1)}, u32[]{:S(2)}, u32[]{:S(2)}) collective-permute-start(f32[256,96]{0,1:T(8,128)S(1)} %add.109), channel_id=1, source_target_pairs={{0,64},{32,96},{64,0},{96,32},{128,192},{160,224},{192,128},{224,1... | collective-permute-start | bytes 294920 | tf_op jit(solution)/shard_map/ppermute | solution.py:25
  111.4 4.8 %collective-permute-done.1 = f32[256,96]{0,1:T(8,128)S(1)} collective-permute-done((f32[256,96]{0,1:T(8,128)S(1)}, f32[256,96]{0,1:T(8,128)S(1)}, u32[]{:S(2)}, u32[]{:S(2)}) %collective-permute-start.1) | collective-permute-done | bytes 98336 | tf_op jit(solution)/shard_map/ppermute | solution.py:25
  116.3 6.3 %collective-permute-start.2 = (f32[256,96]{0,1:T(8,128)S(1)}, f32[256,96]{0,1:T(8,128)S(1)}, u32[]{:S(2)}, u32[]{:S(2)}) collective-permute-start(f32[256,96]{0,1:T(8,128)S(1)} %add.110), channel_id=1, source_target_pairs={{0,128},{32,160},{64,192},{96,224},{128,0},{160,32},{192,64},{224,... | collective-permute-start | bytes 294920 | tf_op jit(solution)/shard_map/ppermute | solution.py:25
  122.5 3.6 %collective-permute-done.2 = f32[256,96]{0,1:T(8,128)S(1)} collective-permute-done((f32[256,96]{0,1:T(8,128)S(1)}, f32[256,96]{0,1:T(8,128)S(1)}, u32[]{:S(2)}, u32[]{:S(2)}) %collective-permute-start.2) | collective-permute-done | bytes 98336 | tf_op jit(solution)/shard_map/ppermute | solution.py:25
  127.2 34.6 %all_to_all.15 = f32[32,8,2049]{2,1,0:T(8,128)S(1)} all-to-all(f32[32,8,2049]{2,1,0:T(8,128)S(1)} %pad_maximum_fusion), channel_id=1, replica_groups=mesh['kv'=8,'blk'=32] {'blk'}, dimensions={0} | all-to-all | bytes 4196352 | tf_op jit(solution)/shard_map/all_to_all | solution.py:40
  162.1 23.3 %all_gather.11 = bf16[256,1024]{1,0:T(8,128)(2,1)S(1)} all-gather(bf16[8,1024]{1,0:T(8,128)(2,1)S(1)} %fusion.28), channel_id=1, replica_groups=mesh['kv'=8,'blk'=32] {'blk'}, dimensions={0}, use_global_device_ids=true | all-gather | bytes 540672 | tf_op jit(solution)/shard_map/all_gather | solution.py:209
  185.9 5.0 %collective-permute-done.3 = f32[256,96]{0,1:T(8,128)S(1)} collective-permute-done((f32[256,96]{0,1:T(8,128)S(1)}, f32[256,96]{0,1:T(8,128)S(1)}, u32[]{:S(2)}, u32[]{:S(2)}) %collective-permute-start.3) | collective-permute-done | bytes 98336 | tf_op jit(solution)/shard_map/ppermute | solution.py:25
  190.9 3.3 %collective-permute-start.4 = (f32[256,96]{0,1:T(8,128)S(1)}, f32[256,96]{0,1:T(8,128)S(1)}, u32[]{:S(2)}, u32[]{:S(2)}) collective-permute-start(f32[256,96]{0,1:T(8,128)S(1)} %add.115), channel_id=1, source_target_pairs={{0,64},{32,96},{64,0},{96,32},{128,192},{160,224},{192,128},{224,1... | collective-permute-start | bytes 294920 | tf_op jit(solution)/shard_map/ppermute | solution.py:25
  194.2 4.8 %collective-permute-done.4 = f32[256,96]{0,1:T(8,128)S(1)} collective-permute-done((f32[256,96]{0,1:T(8,128)S(1)}, f32[256,96]{0,1:T(8,128)S(1)}, u32[]{:S(2)}, u32[]{:S(2)}) %collective-permute-start.4) | collective-permute-done | bytes 98336 | tf_op jit(solution)/shard_map/ppermute | solution.py:25
  199.0 4.3 %collective-permute-start.5 = (f32[256,96]{0,1:T(8,128)S(1)}, f32[256,96]{0,1:T(8,128)S(1)}, u32[]{:S(2)}, u32[]{:S(2)}) collective-permute-start(f32[256,96]{0,1:T(8,128)S(1)} %add.116), channel_id=1, source_target_pairs={{0,128},{32,160},{64,192},{96,224},{128,0},{160,32},{192,64},{224,... | collective-permute-start | bytes 294920 | tf_op jit(solution)/shard_map/ppermute | solution.py:25
  203.4 6.2 %collective-permute-done.5 = f32[256,96]{0,1:T(8,128)S(1)} collective-permute-done((f32[256,96]{0,1:T(8,128)S(1)}, f32[256,96]{0,1:T(8,128)S(1)}, u32[]{:S(2)}, u32[]{:S(2)}) %collective-permute-start.5) | collective-permute-done | bytes 98336 | tf_op jit(solution)/shard_map/ppermute | solution.py:25
  (111 shorter events, 14.0 us)
Async XLA Ops:
  0.6 48.4 %copy-start = (bf16[8,1,128,128]{3,2,1,0:T(8,128)(2,1)S(1)}, bf16[8,1,128,128]{3,2,1,0:T(8,128)(2,1)}, u32[]{:S(2)}) copy-start(bf16[8,1,128,128]{3,2,1,0:T(8,128)(2,1)} %param.30) | copy-start | bytes 786436
  0.6 11.8 %copy-start.12 = (s32[32]{0:T(128)S(1)}, s32[32]{0:T(128)}, u32[]{:S(2)}) copy-start(s32[32]{0:T(128)} %param.35) | copy-start | bytes 388
  0.7 12.0 %copy-start.14 = (s32[8]{0:T(128)S(1)}, s32[8]{0:T(128)}, u32[]{:S(2)}) copy-start(s32[8]{0:T(128)} %param.37) | copy-start | bytes 100
  0.7 12.0 %copy-start.15 = (s32[1,8]{1,0:T(1,128)S(1)}, s32[1,8]{1,0:T(1,128)}, u32[]{:S(2)}) copy-start(s32[1,8]{1,0:T(1,128)} %param.34) | copy-start | bytes 100
  0.7 12.1 %copy-start.6 = (bf16[8,1,127,128]{3,0,2,1:T(8,128)(2,1)S(1)}, bf16[8,1,127,128]{3,0,2,1:T(8,128)(2,1)}, u32[]{:S(2)}) copy-start(bf16[8,1,127,128]{3,0,2,1:T(8,128)(2,1)} %param.32) | copy-start | bytes 780292
  0.7 12.1 %copy-start.7 = (bf16[8,1,127,128]{3,0,2,1:T(8,128)(2,1)S(1)}, bf16[8,1,127,128]{3,0,2,1:T(8,128)(2,1)}, u32[]{:S(2)}) copy-start(bf16[8,1,127,128]{3,0,2,1:T(8,128)(2,1)} %param.33) | copy-start | bytes 780292
  2.7 10.5 %copy-start.16 = (s32[5]{0:T(128)S(1)}, s32[5]{0:T(128)}, u32[]{:S(2)}) copy-start(s32[5]{0:T(128)} %param.36) | copy-start | bytes 64
  4.8 20.9 %all-to-all-start = ((f32[32,8,641]{2,1,0:T(8,128)}), f32[32,8,641]{2,1,0:T(8,128)S(1)}, u32[]{:S(2)}, u32[]{:S(2)}) async-start(f32[32,8,641]{2,1,0:T(8,128)} %pad_maximum_fusion.1), calls=%async_computation | async-start | bytes 1572864 | tf_op jit(solution)/shard_map/all_to_all | solution.py:40
  54.7 9.7 %copy-start.1 = (bf16[8,1,128,128]{3,2,0,1:T(8,128)(2,1)S(1)}, bf16[8,1,128,128]{3,2,0,1:T(8,128)(2,1)}, u32[]{:S(2)}) copy-start(bf16[8,1,128,128]{3,2,0,1:T(8,128)(2,1)} %get-tuple-element.66) | copy-start | bytes 786436
  58.5 44.1 %copy-start.11 = (bf16[384,96]{0,1:T(8,128)(2,1)S(1)}, bf16[384,96]{0,1:T(8,128)(2,1)}, u32[]{:S(2)}) copy-start(bf16[384,96]{0,1:T(8,128)(2,1)} %param.25) | copy-start | bytes 221188
  58.5 67.7 %copy-start.3 = (bf16[1,256,96]{1,2,0:T(8,128)(2,1)S(1)}, bf16[1,256,96]{1,2,0:T(8,128)(2,1)}, u32[]{:S(2)}) copy-start(bf16[1,256,96]{1,2,0:T(8,128)(2,1)} %param.22) | copy-start | bytes 147460
  58.5 68.0 %copy-start.8 = (bf16[96,1024]{1,0:T(8,128)(2,1)S(1)}, bf16[96,1024]{1,0:T(8,128)(2,1)}, u32[]{:S(2)}) copy-start(bf16[96,1024]{1,0:T(8,128)(2,1)} %param.28) | copy-start | bytes 589828
  58.5 68.0 %copy-start.9 = (bf16[96,1024]{1,0:T(8,128)(2,1)S(1)}, bf16[96,1024]{1,0:T(8,128)(2,1)}, u32[]{:S(2)}) copy-start(bf16[96,1024]{1,0:T(8,128)(2,1)} %param.27) | copy-start | bytes 589828
  58.5 68.0 %copy-start.13 = (f32[96]{0:T(128)S(1)}, f32[96]{0:T(128)}, u32[]{:S(2)}) copy-start(f32[96]{0:T(128)} %param.26) | copy-start | bytes 1156
  58.5 19.0 %all-to-all-start.1 = ((f32[32,8,1,3,130]{4,1,3,2,0:T(8,128)}), f32[32,8,1,3,130]{4,1,3,2,0:T(8,128)S(1)}, u32[]{:S(2)}, u32[]{:S(2)}) async-start(f32[32,8,1,3,130]{4,1,3,2,0:T(8,128)} %maximum_bitcast_fusion), calls=%async_computation.1 | async-start | bytes 1572864 | tf_op jit(solution)/shard_map/all_to_all | solution.py:156
  64.5 62.5 %copy-start.2 = (bf16[8,1,128,128]{3,2,0,1:T(8,128)(2,1)}, bf16[8,1,128,128]{3,2,0,1:T(8,128)(2,1)S(1)}, u32[]{:S(2)}) copy-start(bf16[8,1,128,128]{3,2,0,1:T(8,128)(2,1)S(1)} %scatter.6) | copy-start | bytes 786436
  65.0 62.0 %copy-start.5 = (bf16[8,1,128,128]{3,2,0,1:T(8,128)(2,1)}, bf16[8,1,128,128]{3,2,0,1:T(8,128)(2,1)S(1)}, u32[]{:S(2)}) copy-start(bf16[8,1,128,128]{3,2,0,1:T(8,128)(2,1)S(1)} %scatter.9) | copy-start | bytes 786436
  102.8 5.3 %collective-permute-start = (f32[256,96]{0,1:T(8,128)S(1)}, f32[256,96]{0,1:T(8,128)S(1)}, u32[]{:S(2)}, u32[]{:S(2)}) collective-permute-start(f32[256,96]{0,1:T(8,128)S(1)} %fusion.62), channel_id=1, source_target_pairs={{0,32},{32,0},{64,96},{96,64},{128,160},{160,128},{192,224},{224,1... | collective-permute-start | bytes 294920 | tf_op jit(solution)/shard_map/ppermute | solution.py:25
  108.1 8.2 %collective-permute-start.1 = (f32[256,96]{0,1:T(8,128)S(1)}, f32[256,96]{0,1:T(8,128)S(1)}, u32[]{:S(2)}, u32[]{:S(2)}) collective-permute-start(f32[256,96]{0,1:T(8,128)S(1)} %add.109), channel_id=1, source_target_pairs={{0,64},{32,96},{64,0},{96,32},{128,192},{160,224},{192,128},{224,1... | collective-permute-start | bytes 294920 | tf_op jit(solution)/shard_map/ppermute | solution.py:25
  116.3 9.9 %collective-permute-start.2 = (f32[256,96]{0,1:T(8,128)S(1)}, f32[256,96]{0,1:T(8,128)S(1)}, u32[]{:S(2)}, u32[]{:S(2)}) collective-permute-start(f32[256,96]{0,1:T(8,128)S(1)} %add.110), channel_id=1, source_target_pairs={{0,128},{32,160},{64,192},{96,224},{128,0},{160,32},{192,64},{224,... | collective-permute-start | bytes 294920 | tf_op jit(solution)/shard_map/ppermute | solution.py:25
  127.2 58.3 %copy-start.10 = (bf16[1024,96]{0,1:T(8,128)(2,1)S(1)}, bf16[1024,96]{0,1:T(8,128)(2,1)}, u32[]{:S(2)}) copy-start(bf16[1024,96]{0,1:T(8,128)(2,1)} %param.29) | copy-start | bytes 589828
  185.8 5.1 %collective-permute-start.3 = (f32[256,96]{0,1:T(8,128)S(1)}, f32[256,96]{0,1:T(8,128)S(1)}, u32[]{:S(2)}, u32[]{:S(2)}) collective-permute-start(f32[256,96]{0,1:T(8,128)S(1)} %fusion.63), channel_id=1, source_target_pairs={{0,32},{32,0},{64,96},{96,64},{128,160},{160,128},{192,224},{224,1... | collective-permute-start | bytes 294920 | tf_op jit(solution)/shard_map/ppermute | solution.py:25
  190.9 8.1 %collective-permute-start.4 = (f32[256,96]{0,1:T(8,128)S(1)}, f32[256,96]{0,1:T(8,128)S(1)}, u32[]{:S(2)}, u32[]{:S(2)}) collective-permute-start(f32[256,96]{0,1:T(8,128)S(1)} %add.115), channel_id=1, source_target_pairs={{0,64},{32,96},{64,0},{96,32},{128,192},{160,224},{192,128},{224,1... | collective-permute-start | bytes 294920 | tf_op jit(solution)/shard_map/ppermute | solution.py:25
  199.0 10.6 %collective-permute-start.5 = (f32[256,96]{0,1:T(8,128)S(1)}, f32[256,96]{0,1:T(8,128)S(1)}, u32[]{:S(2)}, u32[]{:S(2)}) collective-permute-start(f32[256,96]{0,1:T(8,128)S(1)} %add.116), channel_id=1, source_target_pairs={{0,128},{32,160},{64,192},{96,224},{128,0},{160,32},{192,64},{224,... | collective-permute-start | bytes 294920 | tf_op jit(solution)/shard_map/ppermute | solution.py:25
  (1 other events, 9.6 us)

commit v2 on v1

--- a/solution.py
+++ b/solution.py
@@ -38,6 +38,13 @@
     count = lax.axis_size(axis)
     pieces = value.reshape((count, value.shape[0] // count) + value.shape[1:])
     return jnp.sum(lax.all_to_all(pieces, axis, 0, 0, tiled=False), axis=0)
+
+
+def gather_rows(value, axis):
+    count = lax.axis_size(axis)
+    flat = jnp.broadcast_to(value.reshape(1, -1), (count, value.size))
+    gathered = lax.all_to_all(flat, axis, 0, 0, tiled=False)
+    return gathered.reshape((count * value.shape[0],) + value.shape[1:])
 
 
 def rotate(values, angles):
@@ -124,7 +131,7 @@
     own_queries = rotate(own_proj[:, :, :group_queries], own_angle[:, None, None, :]).astype(
         jnp.bfloat16
     )
-    query_rows = lax.all_gather(own_queries, "blk", axis=0, tiled=True)
+    query_rows = gather_rows(own_queries, "blk")
     new_key = rotate(own_proj[:, :, group_queries], own_angle[:, None, :]).astype(jnp.bfloat16)
     new_value = own_proj[:, :, group_queries + 1].astype(jnp.bfloat16)
     parent_rows = base_rows + parents[0]
@@ -150,10 +157,10 @@
     )
     summed = summed.reshape(heads_kv, all_rows, group_queries, HEAD_WIDTH)
     packed = jnp.concatenate([summed, top_score[..., None], total_mass[..., None]], axis=3)
-    packed = packed.transpose(1, 0, 2, 3).reshape(
+    packed = packed.transpose(1, 0, 2, 3).reshape(blocks, -1)
+    parts = lax.all_to_all(packed, "blk", 0, 0, tiled=False).reshape(
         blocks, own_rows, heads_kv, group_queries, HEAD_WIDTH + 2
     )
-    parts = lax.all_to_all(packed, "blk", 0, 0, tiled=False)
     part_top = parts[..., HEAD_WIDTH]
     prompt_top = jnp.max(part_top, axis=0)
     part_factor = jnp.exp(part_top - prompt_top[None])
@@ -187,7 +194,7 @@
         .astype(jnp.bfloat16)
     )
     head_part = jnp.dot(
-        lax.all_gather(heads_out, "blk", axis=0, tiled=True),
+        gather_rows(heads_out, "blk"),
         w_out,
         preferred_element_type=jnp.float32,
     )
@@ -206,7 +213,7 @@
     upper = mixed[:, unit_count : 2 * unit_count] * own_inverse[:, None]
     hidden = (jax.nn.silu(gate) * upper).astype(jnp.bfloat16)
     ff_part = jnp.dot(
-        lax.all_gather(hidden, "blk", axis=0, tiled=True),
+        gather_rows(hidden, "blk"),
         w_down,
         preferred_element_type=jnp.float32,
     )

time: 211 us -> 192 us (0.910)
  blocking collectives: 104 us -> 61.3 us
  other arithmetic: 10.9 us -> 20.6 us
  local copies, waits for them, and re-layouts: 5.57 us -> 12.7 us
  starting transfers between devices: 32.7 us -> 37.2 us
  waiting for transfers between devices: 49.7 us -> 53.3 us
    all_gather x3 -> x0, blocking collectives: 69.3 us -> none  [the longest x1 23.3 us: body(): lax.all_gather(hidden, 'blk', axis=0, tiled=True)]
    all_to_all x0 -> x2, blocking collectives: none -> 26.8 us  [gather_rows(): gathered = lax.all_to_all(flat, axis, 0, 0, tiled=False)]
    broadcast_in_dim x0 -> x3, other arithmetic: none -> 7.37 us  [gather_rows(): flat = jnp.broadcast_to(value.reshape(1, -1), (count, value.size))]
    all_to_all x0 -> x4, other arithmetic: none -> 6.41 us  [the longest x3 5.44 us: gather_rows(): gathered = lax.all_to_all(flat, axis, 0, 0, tiled=False)]
    all_to_all x1 -> x2, starting transfers between devices: 5.71 us -> 10.1 us  [the longest x1 5.07 us: body(): lax.all_to_all(packed, 'blk', 0, 0, tiled=False)]
    another operation x2 -> x1, other arithmetic: 3.19 us -> 0.02 us
    all_to_all x1 -> x2, waiting for transfers between devices: 12.5 us -> 15.5 us  [the longest x1 8.42 us: body(): lax.all_to_all(packed, 'blk', 0, 0, tiled=False)]
  transfers between devices with their start and end apart: 8 -> 9, of which waited for: 8 -> 9; matrix products, arithmetic and copies ran while one was open for 2% -> 2% of each run, Pallas kernels for 0% -> 0%
where the time goes in v2:
time: 192 us; the launch traced here: 191 us
  blocking collectives  61.3 us (32%)
  waiting for transfers between devices  53.3 us (28%)
  starting transfers between devices  37.2 us (19%)
  other arithmetic  20.6 us (11%)
  local copies, waits for them, and re-layouts  12.7 us (7%)
  matrix products  4.57 us (2%)
    all_to_all x1, blocking collectives, scatter_sum(): return jnp.sum(lax.all_to_all(pieces, axis, 0, 0, tiled=False), axis=0)  34.4 us
    ppermute x6, waiting for transfers between devices, exchange(): return lax.ppermute(value, axis, [(i, i ^ 1 << bit) for i in range(count)])  27 us
    all_to_all x2, blocking collectives, gather_rows(): gathered = lax.all_to_all(flat, axis, 0, 0, tiled=False)  26.8 us
    ppermute x6, starting transfers between devices, exchange(): return lax.ppermute(value, axis, [(i, i ^ 1 << bit) for i in range(count)])  19.5 us
    all_to_all x1, waiting for transfers between devices, scatter_sum(): return jnp.sum(lax.all_to_all(pieces, axis, 0, 0, tiled=False), axis=0)  10.8 us
    all_to_all x1, waiting for transfers between devices, body(): lax.all_to_all(packed, 'blk', 0, 0, tiled=False)  8.42 us
    all_to_all x1, starting transfers between devices, scatter_sum(): return jnp.sum(lax.all_to_all(pieces, axis, 0, 0, tiled=False), axis=0)  7.62 us
    broadcast_in_dim x3, other arithmetic, gather_rows(): flat = jnp.broadcast_to(value.reshape(1, -1), (count, value.size))  7.37 us
  transfers between devices with their start and end apart: 9, of which 9 were waited for; matrix products, arithmetic and copies ran while one was open for 2% of the time, Pallas kernels for 0%

profile of v2, /device:TPU:2, one launch (start us, length us, event | category | flops | bytes accessed | tf_op | source)
XLA Modules:
  0.0 191.0 jit_solution(8109030071032253510)
XLA Ops:
  4.8 7.6 %all-to-all-start = ((f32[32,8,641]{2,1,0:T(8,128)}), f32[32,8,641]{2,1,0:T(8,128)S(1)}, u32[]{:S(2)}, u32[]{:S(2)}) async-start(f32[32,8,641]{2,1,0:T(8,128)} %pad_maximum_fusion.1), calls=%async_computation | async-start | bytes 1572864 | tf_op jit(solution)/shard_map/all_to_all | solution.py:40
  15.0 10.8 %all-to-all-done = f32[32,8,641]{2,1,0:T(8,128)S(1)} async-done(((f32[32,8,641]{2,1,0:T(8,128)}), f32[32,8,641]{2,1,0:T(8,128)S(1)}, u32[]{:S(2)}, u32[]{:S(2)}) %all-to-all-start) | async-done | bytes 656416 | tf_op jit(solution)/shard_map/all_to_all | solution.py:40
  29.5 5.0 %all-to-all-start.1 = ((bf16[32,2,1536]{2,1,0:T(2,128)(2,1)}), bf16[32,2,1536]{2,1,0:T(2,128)(2,1)S(1)}, u32[]{:S(2)}, u32[]{:S(2)}) async-start(bf16[32,2,1536]{2,1,0:T(2,128)(2,1)} %reshape.652), calls=%async_computation.1 | async-start | bytes 393216 | tf_op jit(solution)/shard_map/all_to_all | solution.py:46
  34.6 7.1 %all-to-all-done.1 = bf16[32,2,1536]{2,1,0:T(2,128)(2,1)S(1)} async-done(((bf16[32,2,1536]{2,1,0:T(2,128)(2,1)}), bf16[32,2,1536]{2,1,0:T(2,128)(2,1)S(1)}, u32[]{:S(2)}, u32[]{:S(2)}) %all-to-all-start.1) | async-done | bytes 196640 | tf_op jit(solution)/shard_map/all_to_all | solution.py:46
  46.6 2.1 %all_to_all.31 = f32[32,1,3120]{2,1,0:T(1,128)} reshape(f32[1,256,3,130]{3,2,1,0:T(4,128)S(1)} %copy.154) | data formatting | bytes 798720 | tf_op jit(solution)/shard_map/all_to_all | solution.py:161
  48.7 5.1 %all-to-all-start.2 = ((f32[32,1,3120]{2,1,0:T(1,128)}), f32[32,1,3120]{2,1,0:T(1,128)S(1)}, u32[]{:S(2)}, u32[]{:S(2)}) async-start(f32[32,1,3120]{2,1,0:T(1,128)} %all_to_all.31), calls=%async_computation.2 | async-start | bytes 819200 | tf_op jit(solution)/shard_map/all_to_all | solution.py:161
  54.7 8.4 %all-to-all-done.2 = f32[32,1,3120]{2,1,0:T(1,128)S(1)} async-done(((f32[32,1,3120]{2,1,0:T(1,128)}), f32[32,1,3120]{2,1,0:T(1,128)S(1)}, u32[]{:S(2)}, u32[]{:S(2)}) %all-to-all-start.2) | async-done | bytes 399392 | tf_op jit(solution)/shard_map/all_to_all | solution.py:161
  68.1 1.8 reduce.25
  70.1 11.7 %all_to_all.38 = bf16[32,2,1536]{2,1,0:T(2,128)(2,1)S(1)} all-to-all(bf16[32,2,1536]{2,1,0:T(2,128)(2,1)S(1)} %reshape.654), channel_id=1, replica_groups=mesh['kv'=8,'blk'=32] {'blk'}, dimensions={0} | all-to-all | bytes 393216 | tf_op jit(solution)/shard_map/all_to_all | solution.py:46
  83.4 2.0 %collective-permute-start = (f32[256,96]{0,1:T(8,128)S(1)}, f32[256,96]{0,1:T(8,128)S(1)}, u32[]{:S(2)}, u32[]{:S(2)}) collective-permute-start(f32[256,96]{0,1:T(8,128)S(1)} %fusion.71), channel_id=1, source_target_pairs={{0,32},{32,0},{64,96},{96,64},{128,160},{160,128},{192,224},{224,1... | collective-permute-start | bytes 294920 | tf_op jit(solution)/shard_map/ppermute | solution.py:25
  85.4 3.4 %collective-permute-done = f32[256,96]{0,1:T(8,128)S(1)} collective-permute-done((f32[256,96]{0,1:T(8,128)S(1)}, f32[256,96]{0,1:T(8,128)S(1)}, u32[]{:S(2)}, u32[]{:S(2)}) %collective-permute-start) | collective-permute-done | bytes 98336 | tf_op jit(solution)/shard_map/ppermute | solution.py:25
  88.8 3.4 %collective-permute-start.1 = (f32[256,96]{0,1:T(8,128)S(1)}, f32[256,96]{0,1:T(8,128)S(1)}, u32[]{:S(2)}, u32[]{:S(2)}) collective-permute-start(f32[256,96]{0,1:T(8,128)S(1)} %add.109), channel_id=1, source_target_pairs={{0,64},{32,96},{64,0},{96,32},{128,192},{160,224},{192,128},{224,1... | collective-permute-start | bytes 294920 | tf_op jit(solution)/shard_map/ppermute | solution.py:25
  92.2 4.9 %collective-permute-done.1 = f32[256,96]{0,1:T(8,128)S(1)} collective-permute-done((f32[256,96]{0,1:T(8,128)S(1)}, f32[256,96]{0,1:T(8,128)S(1)}, u32[]{:S(2)}, u32[]{:S(2)}) %collective-permute-start.1) | collective-permute-done | bytes 98336 | tf_op jit(solution)/shard_map/ppermute | solution.py:25
  97.0 6.4 %collective-permute-start.2 = (f32[256,96]{0,1:T(8,128)S(1)}, f32[256,96]{0,1:T(8,128)S(1)}, u32[]{:S(2)}, u32[]{:S(2)}) collective-permute-start(f32[256,96]{0,1:T(8,128)S(1)} %add.110), channel_id=1, source_target_pairs={{0,128},{32,160},{64,192},{96,224},{128,0},{160,32},{192,64},{224,... | collective-permute-start | bytes 294920 | tf_op jit(solution)/shard_map/ppermute | solution.py:25
  103.4 2.6 %collective-permute-done.2 = f32[256,96]{0,1:T(8,128)S(1)} collective-permute-done((f32[256,96]{0,1:T(8,128)S(1)}, f32[256,96]{0,1:T(8,128)S(1)}, u32[]{:S(2)}, u32[]{:S(2)}) %collective-permute-start.2) | collective-permute-done | bytes 98336 | tf_op jit(solution)/shard_map/ppermute | solution.py:25
  107.0 34.4 %all_to_all.39 = f32[32,8,2049]{2,1,0:T(8,128)S(1)} all-to-all(f32[32,8,2049]{2,1,0:T(8,128)S(1)} %pad_maximum_fusion), channel_id=1, replica_groups=mesh['kv'=8,'blk'=32] {'blk'}, dimensions={0} | all-to-all | bytes 4196352 | tf_op jit(solution)/shard_map/all_to_all | solution.py:40
  142.7 3.8 %reduce.26 = bf16[32,8192]{1,0:T(8,128)(2,1)S(1)} reduce(bf16[32,1,8192]{2,1,0:T(2,128)(2,1)S(1)} %broadcast_in_dim.117, bf16[]{:T(256)} %broadcast.364), dimensions={1}, to_apply=%broadcast_in_dim.117.reduce_sub_computation | reduce | bytes 1048578 | tf_op jit(solution)/shard_map/broadcast_in_dim | solution.py:45
  146.9 15.1 %all_to_all.40 = bf16[32,2,4096]{2,1,0:T(2,128)(2,1)S(1)} all-to-all(bf16[32,2,4096]{2,1,0:T(2,128)(2,1)S(1)} %reshape.656), channel_id=1, replica_groups=mesh['kv'=8,'blk'=32] {'blk'}, dimensions={0} | all-to-all | bytes 1048576 | tf_op jit(solution)/shard_map/all_to_all | solution.py:46
  162.6 3.2 %reduce.21 = bf16[32,8192]{1,0:T(8,128)(2,1)S(1)} reduce(bf16[32,1,8192]{2,1,0:T(2,128)(2,1)S(1)} %reshape.657, bf16[]{:T(256)} %constant.156), dimensions={1}, to_apply=%all_to_all.30.reduce_sub_computation | reduce | bytes 1048578 | tf_op jit(solution)/shard_map/all_to_all | solution.py:46
  166.4 5.0 %collective-permute-done.3 = f32[256,96]{0,1:T(8,128)S(1)} collective-permute-done((f32[256,96]{0,1:T(8,128)S(1)}, f32[256,96]{0,1:T(8,128)S(1)}, u32[]{:S(2)}, u32[]{:S(2)}) %collective-permute-start.3) | collective-permute-done | bytes 98336 | tf_op jit(solution)/shard_map/ppermute | solution.py:25
  171.5 3.2 %collective-permute-start.4 = (f32[256,96]{0,1:T(8,128)S(1)}, f32[256,96]{0,1:T(8,128)S(1)}, u32[]{:S(2)}, u32[]{:S(2)}) collective-permute-start(f32[256,96]{0,1:T(8,128)S(1)} %add.115), channel_id=1, source_target_pairs={{0,64},{32,96},{64,0},{96,32},{128,192},{160,224},{192,128},{224,1... | collective-permute-start | bytes 294920 | tf_op jit(solution)/shard_map/ppermute | solution.py:25
  174.7 4.9 %collective-permute-done.4 = f32[256,96]{0,1:T(8,128)S(1)} collective-permute-done((f32[256,96]{0,1:T(8,128)S(1)}, f32[256,96]{0,1:T(8,128)S(1)}, u32[]{:S(2)}, u32[]{:S(2)}) %collective-permute-start.4) | collective-permute-done | bytes 98336 | tf_op jit(solution)/shard_map/ppermute | solution.py:25
  179.6 4.5 %collective-permute-start.5 = (f32[256,96]{0,1:T(8,128)S(1)}, f32[256,96]{0,1:T(8,128)S(1)}, u32[]{:S(2)}, u32[]{:S(2)}) collective-permute-start(f32[256,96]{0,1:T(8,128)S(1)} %add.116), channel_id=1, source_target_pairs={{0,128},{32,160},{64,192},{96,224},{128,0},{160,32},{192,64},{224,... | collective-permute-start | bytes 294920 | tf_op jit(solution)/shard_map/ppermute | solution.py:25
  184.1 6.2 %collective-permute-done.5 = f32[256,96]{0,1:T(8,128)S(1)} collective-permute-done((f32[256,96]{0,1:T(8,128)S(1)}, f32[256,96]{0,1:T(8,128)S(1)}, u32[]{:S(2)}, u32[]{:S(2)}) %collective-permute-start.5) | collective-permute-done | bytes 98336 | tf_op jit(solution)/shard_map/ppermute | solution.py:25
  (130 shorter events, 27.1 us)
Async XLA Ops:
  0.6 42.6 %copy-start = (bf16[8,1,128,128]{3,2,1,0:T(8,128)(2,1)S(1)}, bf16[8,1,128,128]{3,2,1,0:T(8,128)(2,1)}, u32[]{:S(2)}) copy-start(bf16[8,1,128,128]{3,2,1,0:T(8,128)(2,1)} %param.30) | copy-start | bytes 786436
  0.6 11.8 %copy-start.13 = (s32[1,8]{1,0:T(1,128)S(1)}, s32[1,8]{1,0:T(1,128)}, u32[]{:S(2)}) copy-start(s32[1,8]{1,0:T(1,128)} %param.34) | copy-start | bytes 100
  0.7 11.9 %copy-start.14 = (s32[8]{0:T(128)S(1)}, s32[8]{0:T(128)}, u32[]{:S(2)}) copy-start(s32[8]{0:T(128)} %param.37) | copy-start | bytes 100
  0.7 11.9 %copy-start.10 = (s32[32]{0:T(128)S(1)}, s32[32]{0:T(128)}, u32[]{:S(2)}) copy-start(s32[32]{0:T(128)} %param.35) | copy-start | bytes 388
  0.7 12.1 %copy-start.4 = (bf16[8,1,127,128]{3,0,2,1:T(8,128)(2,1)S(1)}, bf16[8,1,127,128]{3,0,2,1:T(8,128)(2,1)}, u32[]{:S(2)}) copy-start(bf16[8,1,127,128]{3,0,2,1:T(8,128)(2,1)} %param.32) | copy-start | bytes 780292
  0.7 12.1 %copy-start.5 = (bf16[8,1,127,128]{3,0,2,1:T(8,128)(2,1)S(1)}, bf16[8,1,127,128]{3,0,2,1:T(8,128)(2,1)}, u32[]{:S(2)}) copy-start(bf16[8,1,127,128]{3,0,2,1:T(8,128)(2,1)} %param.33) | copy-start | bytes 780292
  2.7 10.5 %copy-start.15 = (s32[5]{0:T(128)S(1)}, s32[5]{0:T(128)}, u32[]{:S(2)}) copy-start(s32[5]{0:T(128)} %param.36) | copy-start | bytes 64
  4.8 20.9 %all-to-all-start = ((f32[32,8,641]{2,1,0:T(8,128)}), f32[32,8,641]{2,1,0:T(8,128)S(1)}, u32[]{:S(2)}, u32[]{:S(2)}) async-start(f32[32,8,641]{2,1,0:T(8,128)} %pad_maximum_fusion.1), calls=%async_computation | async-start | bytes 1572864 | tf_op jit(solution)/shard_map/all_to_all | solution.py:40
  29.5 12.1 %all-to-all-start.1 = ((bf16[32,2,1536]{2,1,0:T(2,128)(2,1)}), bf16[32,2,1536]{2,1,0:T(2,128)(2,1)S(1)}, u32[]{:S(2)}, u32[]{:S(2)}) async-start(bf16[32,2,1536]{2,1,0:T(2,128)(2,1)} %reshape.652), calls=%async_computation.1 | async-start | bytes 393216 | tf_op jit(solution)/shard_map/all_to_all | solution.py:46
  48.7 14.4 %all-to-all-start.2 = ((f32[32,1,3120]{2,1,0:T(1,128)}), f32[32,1,3120]{2,1,0:T(1,128)S(1)}, u32[]{:S(2)}, u32[]{:S(2)}) async-start(f32[32,1,3120]{2,1,0:T(1,128)} %all_to_all.31), calls=%async_computation.2 | async-start | bytes 819200 | tf_op jit(solution)/shard_map/all_to_all | solution.py:161
  54.0 13.6 %copy-start.3 = (bf16[8,1,128,128]{3,2,0,1:T(8,128)(2,1)}, bf16[8,1,128,128]{3,2,0,1:T(8,128)(2,1)S(1)}, u32[]{:S(2)}) copy-start(bf16[8,1,128,128]{3,2,0,1:T(8,128)(2,1)S(1)} %scatter.9) | copy-start | bytes 786436
  54.3 13.2 %copy-start.1 = (bf16[8,1,128,128]{3,2,0,1:T(8,128)(2,1)}, bf16[8,1,128,128]{3,2,0,1:T(8,128)(2,1)S(1)}, u32[]{:S(2)}) copy-start(bf16[8,1,128,128]{3,2,0,1:T(8,128)(2,1)S(1)} %scatter.6) | copy-start | bytes 786436
  65.9 17.3 %copy-start.9 = (bf16[384,96]{0,1:T(8,128)(2,1)S(1)}, bf16[384,96]{0,1:T(8,128)(2,1)}, u32[]{:S(2)}) copy-start(bf16[384,96]{0,1:T(8,128)(2,1)} %param.25) | copy-start | bytes 221188
  66.3 39.7 %copy-start.2 = (bf16[1,256,96]{1,2,0:T(8,128)(2,1)S(1)}, bf16[1,256,96]{1,2,0:T(8,128)(2,1)}, u32[]{:S(2)}) copy-start(bf16[1,256,96]{1,2,0:T(8,128)(2,1)} %param.22) | copy-start | bytes 147460
  66.6 39.6 %copy-start.6 = (bf16[96,1024]{1,0:T(8,128)(2,1)S(1)}, bf16[96,1024]{1,0:T(8,128)(2,1)}, u32[]{:S(2)}) copy-start(bf16[96,1024]{1,0:T(8,128)(2,1)} %param.28) | copy-start | bytes 589828
  66.6 39.6 %copy-start.7 = (bf16[96,1024]{1,0:T(8,128)(2,1)S(1)}, bf16[96,1024]{1,0:T(8,128)(2,1)}, u32[]{:S(2)}) copy-start(bf16[96,1024]{1,0:T(8,128)(2,1)} %param.27) | copy-start | bytes 589828
  66.6 39.6 %copy-start.11 = (f32[96]{0:T(128)S(1)}, f32[96]{0:T(128)}, u32[]{:S(2)}) copy-start(f32[96]{0:T(128)} %param.26) | copy-start | bytes 1156
  83.4 5.4 %collective-permute-start = (f32[256,96]{0,1:T(8,128)S(1)}, f32[256,96]{0,1:T(8,128)S(1)}, u32[]{:S(2)}, u32[]{:S(2)}) collective-permute-start(f32[256,96]{0,1:T(8,128)S(1)} %fusion.71), channel_id=1, source_target_pairs={{0,32},{32,0},{64,96},{96,64},{128,160},{160,128},{192,224},{224,1... | collective-permute-start | bytes 294920 | tf_op jit(solution)/shard_map/ppermute | solution.py:25
  88.8 8.2 %collective-permute-start.1 = (f32[256,96]{0,1:T(8,128)S(1)}, f32[256,96]{0,1:T(8,128)S(1)}, u32[]{:S(2)}, u32[]{:S(2)}) collective-permute-start(f32[256,96]{0,1:T(8,128)S(1)} %add.109), channel_id=1, source_target_pairs={{0,64},{32,96},{64,0},{96,32},{128,192},{160,224},{192,128},{224,1... | collective-permute-start | bytes 294920 | tf_op jit(solution)/shard_map/ppermute | solution.py:25
  97.0 9.0 %collective-permute-start.2 = (f32[256,96]{0,1:T(8,128)S(1)}, f32[256,96]{0,1:T(8,128)S(1)}, u32[]{:S(2)}, u32[]{:S(2)}) collective-permute-start(f32[256,96]{0,1:T(8,128)S(1)} %add.110), channel_id=1, source_target_pairs={{0,128},{32,160},{64,192},{96,224},{128,0},{160,32},{192,64},{224,... | collective-permute-start | bytes 294920 | tf_op jit(solution)/shard_map/ppermute | solution.py:25
  146.5 19.5 %copy-start.8 = (bf16[1024,96]{0,1:T(8,128)(2,1)S(1)}, bf16[1024,96]{0,1:T(8,128)(2,1)}, u32[]{:S(2)}) copy-start(bf16[1024,96]{0,1:T(8,128)(2,1)} %param.29) | copy-start | bytes 589828
  166.3 5.2 %collective-permute-start.3 = (f32[256,96]{0,1:T(8,128)S(1)}, f32[256,96]{0,1:T(8,128)S(1)}, u32[]{:S(2)}, u32[]{:S(2)}) collective-permute-start(f32[256,96]{0,1:T(8,128)S(1)} %fusion.72), channel_id=1, source_target_pairs={{0,32},{32,0},{64,96},{96,64},{128,160},{160,128},{192,224},{224,1... | collective-permute-start | bytes 294920 | tf_op jit(solution)/shard_map/ppermute | solution.py:25
  171.5 8.1 %collective-permute-start.4 = (f32[256,96]{0,1:T(8,128)S(1)}, f32[256,96]{0,1:T(8,128)S(1)}, u32[]{:S(2)}, u32[]{:S(2)}) collective-permute-start(f32[256,96]{0,1:T(8,128)S(1)} %add.115), channel_id=1, source_target_pairs={{0,64},{32,96},{64,0},{96,32},{128,192},{160,224},{192,128},{224,1... | collective-permute-start | bytes 294920 | tf_op jit(solution)/shard_map/ppermute | solution.py:25
  179.6 10.7 %collective-permute-start.5 = (f32[256,96]{0,1:T(8,128)S(1)}, f32[256,96]{0,1:T(8,128)S(1)}, u32[]{:S(2)}, u32[]{:S(2)}) collective-permute-start(f32[256,96]{0,1:T(8,128)S(1)} %add.116), channel_id=1, source_target_pairs={{0,128},{32,160},{64,192},{96,224},{128,0},{160,32},{192,64},{224,... | collective-permute-start | bytes 294920 | tf_op jit(solution)/shard_map/ppermute | solution.py:25
  (1 other events, 1.9 us)

commit v3 on v2

--- a/solution.py
+++ b/solution.py
@@ -34,10 +34,10 @@
     return value
 
 
-def scatter_sum(value, axis):
+def scatter_sum(value, axis, sum_type=None):
     count = lax.axis_size(axis)
     pieces = value.reshape((count, value.shape[0] // count) + value.shape[1:])
-    return jnp.sum(lax.all_to_all(pieces, axis, 0, 0, tiled=False), axis=0)
+    return jnp.sum(lax.all_to_all(pieces, axis, 0, 0, tiled=False).astype(sum_type), axis=0)
 
 
 def gather_rows(value, axis):
@@ -201,14 +201,21 @@
     after_attn = residual + across_heads(head_part)
     squares2 = jnp.sum(after_attn * after_attn, axis=1)
     normed2 = (after_attn * mlp_norm).astype(jnp.bfloat16)
+    squares2_high = squares2.astype(jnp.bfloat16)
+    squares2_low = (squares2 - squares2_high.astype(jnp.float32)).astype(jnp.bfloat16)
     mixed = scatter_sum(
         jnp.concatenate(
-            [jnp.dot(normed2, w_both, preferred_element_type=jnp.float32), squares2[:, None]],
+            [
+                jnp.dot(normed2, w_both, preferred_element_type=jnp.float32).astype(jnp.bfloat16),
+                squares2_high[:, None],
+                squares2_low[:, None],
+            ],
             axis=1,
         ),
         "blk",
-    )
-    own_inverse = lax.rsqrt(mixed[:, -1] / MODEL_WIDTH + 1e-05)
+        jnp.float32,
+    )
+    own_inverse = lax.rsqrt((mixed[:, -2] + mixed[:, -1]) / MODEL_WIDTH + 1e-05)
     gate = mixed[:, :unit_count] * own_inverse[:, None]
     upper = mixed[:, unit_count : 2 * unit_count] * own_inverse[:, None]
     hidden = (jax.nn.silu(gate) * upper).astype(jnp.bfloat16)

time: 192 us -> 181 us (0.943)
  blocking collectives: 61.3 us -> 49.4 us
    all_to_all x1, blocking collectives: 34.4 us -> 22.7 us  [scatter_sum(): lax.all_to_all(pieces, axis, 0, 0, tiled=False).astype(sum_type)]
where the time goes in v3:
time: 181 us; the launch traced here: 180 us
  waiting for transfers between devices  53.3 us (29%)
  blocking collectives  49.4 us (27%)
  starting transfers between devices  37.2 us (21%)
  other arithmetic  20.4 us (11%)
  local copies, waits for them, and re-layouts  14 us (8%)
  matrix products  4.57 us (3%)
    ppermute x6, waiting for transfers between devices, exchange(): return lax.ppermute(value, axis, [(i, i ^ 1 << bit) for i in range(count)])  27 us
    all_to_all x2, blocking collectives, gather_rows(): gathered = lax.all_to_all(flat, axis, 0, 0, tiled=False)  26.7 us
    all_to_all x1, blocking collectives, scatter_sum(): lax.all_to_all(pieces, axis, 0, 0, tiled=False).astype(sum_type)  22.7 us
    ppermute x6, starting transfers between devices, exchange(): return lax.ppermute(value, axis, [(i, i ^ 1 << bit) for i in range(count)])  19.5 us
    all_to_all x1, waiting for transfers between devices, scatter_sum(): lax.all_to_all(pieces, axis, 0, 0, tiled=False).astype(sum_type)  10.8 us
    all_to_all x1, waiting for transfers between devices, body(): lax.all_to_all(packed, 'blk', 0, 0, tiled=False)  8.42 us
    all_to_all x1, starting transfers between devices, scatter_sum(): lax.all_to_all(pieces, axis, 0, 0, tiled=False).astype(sum_type)  7.62 us
    broadcast_in_dim x3, other arithmetic, gather_rows(): flat = jnp.broadcast_to(value.reshape(1, -1), (count, value.size))  7.37 us
  transfers between devices with their start and end apart: 9, of which 9 were waited for; matrix products, arithmetic and copies ran while one was open for 2% of the time, Pallas kernels for 0%

profile of v3, /device:TPU:2, one launch (start us, length us, event | category | flops | bytes accessed | tf_op | source)
XLA Modules:
  0.0 180.3 jit_solution(12809605180585238768)
XLA Ops:
  4.8 7.6 %all-to-all-start = ((f32[32,8,641]{2,1,0:T(8,128)}), f32[32,8,641]{2,1,0:T(8,128)S(1)}, u32[]{:S(2)}, u32[]{:S(2)}) async-start(f32[32,8,641]{2,1,0:T(8,128)} %pad_maximum_fusion), calls=%async_computation | async-start | bytes 1572864 | tf_op jit(solution)/shard_map/all_to_all | solution.py:40
  15.0 10.8 %all-to-all-done = f32[32,8,641]{2,1,0:T(8,128)S(1)} async-done(((f32[32,8,641]{2,1,0:T(8,128)}), f32[32,8,641]{2,1,0:T(8,128)S(1)}, u32[]{:S(2)}, u32[]{:S(2)}) %all-to-all-start) | async-done | bytes 656416 | tf_op jit(solution)/shard_map/all_to_all | solution.py:40
  29.5 5.0 %all-to-all-start.1 = ((bf16[32,2,1536]{2,1,0:T(2,128)(2,1)}), bf16[32,2,1536]{2,1,0:T(2,128)(2,1)S(1)}, u32[]{:S(2)}, u32[]{:S(2)}) async-start(bf16[32,2,1536]{2,1,0:T(2,128)(2,1)} %reshape.683), calls=%async_computation.1 | async-start | bytes 393216 | tf_op jit(solution)/shard_map/all_to_all | solution.py:46
  34.6 7.1 %all-to-all-done.1 = bf16[32,2,1536]{2,1,0:T(2,128)(2,1)S(1)} async-done(((bf16[32,2,1536]{2,1,0:T(2,128)(2,1)}), bf16[32,2,1536]{2,1,0:T(2,128)(2,1)S(1)}, u32[]{:S(2)}, u32[]{:S(2)}) %all-to-all-start.1) | async-done | bytes 196640 | tf_op jit(solution)/shard_map/all_to_all | solution.py:46
  46.6 2.1 %all_to_all.31 = f32[32,1,3120]{2,1,0:T(1,128)} reshape(f32[1,256,3,130]{3,2,1,0:T(4,128)S(1)} %copy.160) | data formatting | bytes 798720 | tf_op jit(solution)/shard_map/all_to_all | solution.py:161
  48.7 5.1 %all-to-all-start.2 = ((f32[32,1,3120]{2,1,0:T(1,128)}), f32[32,1,3120]{2,1,0:T(1,128)S(1)}, u32[]{:S(2)}, u32[]{:S(2)}) async-start(f32[32,1,3120]{2,1,0:T(1,128)} %all_to_all.31), calls=%async_computation.2 | async-start | bytes 819200 | tf_op jit(solution)/shard_map/all_to_all | solution.py:161
  54.7 8.4 %all-to-all-done.2 = f32[32,1,3120]{2,1,0:T(1,128)S(1)} async-done(((f32[32,1,3120]{2,1,0:T(1,128)}), f32[32,1,3120]{2,1,0:T(1,128)S(1)}, u32[]{:S(2)}, u32[]{:S(2)}) %all-to-all-start.2) | async-done | bytes 399392 | tf_op jit(solution)/shard_map/all_to_all | solution.py:161
  68.1 1.8 reduce.25
  70.1 11.7 %all_to_all.38 = bf16[32,2,1536]{2,1,0:T(2,128)(2,1)S(1)} all-to-all(bf16[32,2,1536]{2,1,0:T(2,128)(2,1)S(1)} %reshape.685), channel_id=1, replica_groups=mesh['kv'=8,'blk'=32] {'blk'}, dimensions={0} | all-to-all | bytes 393216 | tf_op jit(solution)/shard_map/all_to_all | solution.py:46
  83.4 2.0 %collective-permute-start = (f32[256,96]{0,1:T(8,128)S(1)}, f32[256,96]{0,1:T(8,128)S(1)}, u32[]{:S(2)}, u32[]{:S(2)}) collective-permute-start(f32[256,96]{0,1:T(8,128)S(1)} %fusion.73), channel_id=1, source_target_pairs={{0,32},{32,0},{64,96},{96,64},{128,160},{160,128},{192,224},{224,1... | collective-permute-start | bytes 294920 | tf_op jit(solution)/shard_map/ppermute | solution.py:25
  85.4 3.4 %collective-permute-done = f32[256,96]{0,1:T(8,128)S(1)} collective-permute-done((f32[256,96]{0,1:T(8,128)S(1)}, f32[256,96]{0,1:T(8,128)S(1)}, u32[]{:S(2)}, u32[]{:S(2)}) %collective-permute-start) | collective-permute-done | bytes 98336 | tf_op jit(solution)/shard_map/ppermute | solution.py:25
  88.8 3.4 %collective-permute-start.1 = (f32[256,96]{0,1:T(8,128)S(1)}, f32[256,96]{0,1:T(8,128)S(1)}, u32[]{:S(2)}, u32[]{:S(2)}) collective-permute-start(f32[256,96]{0,1:T(8,128)S(1)} %add.113), channel_id=1, source_target_pairs={{0,64},{32,96},{64,0},{96,32},{128,192},{160,224},{192,128},{224,1... | collective-permute-start | bytes 294920 | tf_op jit(solution)/shard_map/ppermute | solution.py:25
  92.2 4.9 %collective-permute-done.1 = f32[256,96]{0,1:T(8,128)S(1)} collective-permute-done((f32[256,96]{0,1:T(8,128)S(1)}, f32[256,96]{0,1:T(8,128)S(1)}, u32[]{:S(2)}, u32[]{:S(2)}) %collective-permute-start.1) | collective-permute-done | bytes 98336 | tf_op jit(solution)/shard_map/ppermute | solution.py:25
  97.0 6.4 %collective-permute-start.2 = (f32[256,96]{0,1:T(8,128)S(1)}, f32[256,96]{0,1:T(8,128)S(1)}, u32[]{:S(2)}, u32[]{:S(2)}) collective-permute-start(f32[256,96]{0,1:T(8,128)S(1)} %add.114), channel_id=1, source_target_pairs={{0,128},{32,160},{64,192},{96,224},{128,0},{160,32},{192,64},{224,... | collective-permute-start | bytes 294920 | tf_op jit(solution)/shard_map/ppermute | solution.py:25
  103.4 2.6 %collective-permute-done.2 = f32[256,96]{0,1:T(8,128)S(1)} collective-permute-done((f32[256,96]{0,1:T(8,128)S(1)}, f32[256,96]{0,1:T(8,128)S(1)}, u32[]{:S(2)}, u32[]{:S(2)}) %collective-permute-start.2) | collective-permute-done | bytes 98336 | tf_op jit(solution)/shard_map/ppermute | solution.py:25
  108.0 22.7 %all_to_all.39 = bf16[32,8,2050]{2,1,0:T(8,128)(2,1)S(1)} all-to-all(bf16[32,8,2050]{2,1,0:T(8,128)(2,1)S(1)} %concatenate.73), channel_id=1, replica_groups=mesh['kv'=8,'blk'=32] {'blk'}, dimensions={0} | all-to-all | bytes 2099200 | tf_op jit(solution)/shard_map/all_to_all | solution.py:40
  132.1 3.8 %reduce.26 = bf16[32,8192]{1,0:T(8,128)(2,1)S(1)} reduce(bf16[32,1,8192]{2,1,0:T(2,128)(2,1)S(1)} %broadcast_in_dim.118, bf16[]{:T(256)} %broadcast.364), dimensions={1}, to_apply=%broadcast_in_dim.118.reduce_sub_computation | reduce | bytes 1048578 | tf_op jit(solution)/shard_map/broadcast_in_dim | solution.py:45
  136.3 15.1 %all_to_all.40 = bf16[32,2,4096]{2,1,0:T(2,128)(2,1)S(1)} all-to-all(bf16[32,2,4096]{2,1,0:T(2,128)(2,1)S(1)} %reshape.687), channel_id=1, replica_groups=mesh['kv'=8,'blk'=32] {'blk'}, dimensions={0} | all-to-all | bytes 1048576 | tf_op jit(solution)/shard_map/all_to_all | solution.py:46
  151.9 3.2 %reduce.21 = bf16[32,8192]{1,0:T(8,128)(2,1)S(1)} reduce(bf16[32,1,8192]{2,1,0:T(2,128)(2,1)S(1)} %reshape.688, bf16[]{:T(256)} %constant.156), dimensions={1}, to_apply=%all_to_all.30.reduce_sub_computation | reduce | bytes 1048578 | tf_op jit(solution)/shard_map/all_to_all | solution.py:46
  155.8 5.0 %collective-permute-done.3 = f32[256,96]{0,1:T(8,128)S(1)} collective-permute-done((f32[256,96]{0,1:T(8,128)S(1)}, f32[256,96]{0,1:T(8,128)S(1)}, u32[]{:S(2)}, u32[]{:S(2)}) %collective-permute-start.3) | collective-permute-done | bytes 98336 | tf_op jit(solution)/shard_map/ppermute | solution.py:25
  160.8 3.2 %collective-permute-start.4 = (f32[256,96]{0,1:T(8,128)S(1)}, f32[256,96]{0,1:T(8,128)S(1)}, u32[]{:S(2)}, u32[]{:S(2)}) collective-permute-start(f32[256,96]{0,1:T(8,128)S(1)} %add.120), channel_id=1, source_target_pairs={{0,64},{32,96},{64,0},{96,32},{128,192},{160,224},{192,128},{224,1... | collective-permute-start | bytes 294920 | tf_op jit(solution)/shard_map/ppermute | solution.py:25
  164.0 4.8 %collective-permute-done.4 = f32[256,96]{0,1:T(8,128)S(1)} collective-permute-done((f32[256,96]{0,1:T(8,128)S(1)}, f32[256,96]{0,1:T(8,128)S(1)}, u32[]{:S(2)}, u32[]{:S(2)}) %collective-permute-start.4) | collective-permute-done | bytes 98336 | tf_op jit(solution)/shard_map/ppermute | solution.py:25
  168.9 4.5 %collective-permute-start.5 = (f32[256,96]{0,1:T(8,128)S(1)}, f32[256,96]{0,1:T(8,128)S(1)}, u32[]{:S(2)}, u32[]{:S(2)}) collective-permute-start(f32[256,96]{0,1:T(8,128)S(1)} %add.121), channel_id=1, source_target_pairs={{0,128},{32,160},{64,192},{96,224},{128,0},{160,32},{192,64},{224,... | collective-permute-start | bytes 294920 | tf_op jit(solution)/shard_map/ppermute | solution.py:25
  173.4 6.2 %collective-permute-done.5 = f32[256,96]{0,1:T(8,128)S(1)} collective-permute-done((f32[256,96]{0,1:T(8,128)S(1)}, f32[256,96]{0,1:T(8,128)S(1)}, u32[]{:S(2)}, u32[]{:S(2)}) %collective-permute-start.5) | collective-permute-done | bytes 98336 | tf_op jit(solution)/shard_map/ppermute | solution.py:25
  (134 shorter events, 28.2 us)
Async XLA Ops:
  0.6 42.6 %copy-start = (bf16[8,1,128,128]{3,2,1,0:T(8,128)(2,1)S(1)}, bf16[8,1,128,128]{3,2,1,0:T(8,128)(2,1)}, u32[]{:S(2)}) copy-start(bf16[8,1,128,128]{3,2,1,0:T(8,128)(2,1)} %param.30) | copy-start | bytes 786436
  0.6 11.8 %copy-start.11 = (s32[32]{0:T(128)S(1)}, s32[32]{0:T(128)}, u32[]{:S(2)}) copy-start(s32[32]{0:T(128)} %param.35) | copy-start | bytes 388
  0.7 12.0 %copy-start.13 = (s32[8]{0:T(128)S(1)}, s32[8]{0:T(128)}, u32[]{:S(2)}) copy-start(s32[8]{0:T(128)} %param.37) | copy-start | bytes 100
  0.7 12.0 %copy-start.14 = (s32[1,8]{1,0:T(1,128)S(1)}, s32[1,8]{1,0:T(1,128)}, u32[]{:S(2)}) copy-start(s32[1,8]{1,0:T(1,128)} %param.34) | copy-start | bytes 100
  0.7 12.1 %copy-start.4 = (bf16[8,1,127,128]{3,0,2,1:T(8,128)(2,1)S(1)}, bf16[8,1,127,128]{3,0,2,1:T(8,128)(2,1)}, u32[]{:S(2)}) copy-start(bf16[8,1,127,128]{3,0,2,1:T(8,128)(2,1)} %param.32) | copy-start | bytes 780292
  0.7 12.1 %copy-start.5 = (bf16[8,1,127,128]{3,0,2,1:T(8,128)(2,1)S(1)}, bf16[8,1,127,128]{3,0,2,1:T(8,128)(2,1)}, u32[]{:S(2)}) copy-start(bf16[8,1,127,128]{3,0,2,1:T(8,128)(2,1)} %param.33) | copy-start | bytes 780292
  2.7 10.4 %copy-start.15 = (s32[5]{0:T(128)S(1)}, s32[5]{0:T(128)}, u32[]{:S(2)}) copy-start(s32[5]{0:T(128)} %param.36) | copy-start | bytes 64
  4.8 20.9 %all-to-all-start = ((f32[32,8,641]{2,1,0:T(8,128)}), f32[32,8,641]{2,1,0:T(8,128)S(1)}, u32[]{:S(2)}, u32[]{:S(2)}) async-start(f32[32,8,641]{2,1,0:T(8,128)} %pad_maximum_fusion), calls=%async_computation | async-start | bytes 1572864 | tf_op jit(solution)/shard_map/all_to_all | solution.py:40
  29.5 12.1 %all-to-all-start.1 = ((bf16[32,2,1536]{2,1,0:T(2,128)(2,1)}), bf16[32,2,1536]{2,1,0:T(2,128)(2,1)S(1)}, u32[]{:S(2)}, u32[]{:S(2)}) async-start(bf16[32,2,1536]{2,1,0:T(2,128)(2,1)} %reshape.683), calls=%async_computation.1 | async-start | bytes 393216 | tf_op jit(solution)/shard_map/all_to_all | solution.py:46
  48.7 14.4 %all-to-all-start.2 = ((f32[32,1,3120]{2,1,0:T(1,128)}), f32[32,1,3120]{2,1,0:T(1,128)S(1)}, u32[]{:S(2)}, u32[]{:S(2)}) async-start(f32[32,1,3120]{2,1,0:T(1,128)} %all_to_all.31), calls=%async_computation.2 | async-start | bytes 819200 | tf_op jit(solution)/shard_map/all_to_all | solution.py:161
  54.1 13.4 %copy-start.1 = (bf16[8,1,128,128]{3,2,0,1:T(8,128)(2,1)}, bf16[8,1,128,128]{3,2,0,1:T(8,128)(2,1)S(1)}, u32[]{:S(2)}) copy-start(bf16[8,1,128,128]{3,2,0,1:T(8,128)(2,1)S(1)} %scatter.6) | copy-start | bytes 786436
  54.3 13.3 %copy-start.3 = (bf16[8,1,128,128]{3,2,0,1:T(8,128)(2,1)}, bf16[8,1,128,128]{3,2,0,1:T(8,128)(2,1)S(1)}, u32[]{:S(2)}) copy-start(bf16[8,1,128,128]{3,2,0,1:T(8,128)(2,1)S(1)} %scatter.9) | copy-start | bytes 786436
  65.9 17.3 %copy-start.9 = (bf16[384,96]{0,1:T(8,128)(2,1)S(1)}, bf16[384,96]{0,1:T(8,128)(2,1)}, u32[]{:S(2)}) copy-start(bf16[384,96]{0,1:T(8,128)(2,1)} %param.25) | copy-start | bytes 221188
  66.2 39.8 %copy-start.2 = (bf16[1,256,96]{1,2,0:T(8,128)(2,1)S(1)}, bf16[1,256,96]{1,2,0:T(8,128)(2,1)}, u32[]{:S(2)}) copy-start(bf16[1,256,96]{1,2,0:T(8,128)(2,1)} %param.22) | copy-start | bytes 147460
  66.5 40.0 %copy-start.7 = (bf16[96,1024]{1,0:T(8,128)(2,1)S(1)}, bf16[96,1024]{1,0:T(8,128)(2,1)}, u32[]{:S(2)}) copy-start(bf16[96,1024]{1,0:T(8,128)(2,1)} %param.28) | copy-start | bytes 589828
  66.5 40.0 %copy-start.8 = (bf16[96,1024]{1,0:T(8,128)(2,1)S(1)}, bf16[96,1024]{1,0:T(8,128)(2,1)}, u32[]{:S(2)}) copy-start(bf16[96,1024]{1,0:T(8,128)(2,1)} %param.27) | copy-start | bytes 589828
  66.5 40.0 %copy-start.10 = (f32[96]{0:T(128)S(1)}, f32[96]{0:T(128)}, u32[]{:S(2)}) copy-start(f32[96]{0:T(128)} %param.26) | copy-start | bytes 1156
  83.4 5.4 %collective-permute-start = (f32[256,96]{0,1:T(8,128)S(1)}, f32[256,96]{0,1:T(8,128)S(1)}, u32[]{:S(2)}, u32[]{:S(2)}) collective-permute-start(f32[256,96]{0,1:T(8,128)S(1)} %fusion.73), channel_id=1, source_target_pairs={{0,32},{32,0},{64,96},{96,64},{128,160},{160,128},{192,224},{224,1... | collective-permute-start | bytes 294920 | tf_op jit(solution)/shard_map/ppermute | solution.py:25
  88.8 8.2 %collective-permute-start.1 = (f32[256,96]{0,1:T(8,128)S(1)}, f32[256,96]{0,1:T(8,128)S(1)}, u32[]{:S(2)}, u32[]{:S(2)}) collective-permute-start(f32[256,96]{0,1:T(8,128)S(1)} %add.113), channel_id=1, source_target_pairs={{0,64},{32,96},{64,0},{96,32},{128,192},{160,224},{192,128},{224,1... | collective-permute-start | bytes 294920 | tf_op jit(solution)/shard_map/ppermute | solution.py:25
  97.0 9.0 %collective-permute-start.2 = (f32[256,96]{0,1:T(8,128)S(1)}, f32[256,96]{0,1:T(8,128)S(1)}, u32[]{:S(2)}, u32[]{:S(2)}) collective-permute-start(f32[256,96]{0,1:T(8,128)S(1)} %add.114), channel_id=1, source_target_pairs={{0,128},{32,160},{64,192},{96,224},{128,0},{160,32},{192,64},{224,... | collective-permute-start | bytes 294920 | tf_op jit(solution)/shard_map/ppermute | solution.py:25
  135.9 19.4 %copy-start.6 = (bf16[1024,96]{0,1:T(8,128)(2,1)S(1)}, bf16[1024,96]{0,1:T(8,128)(2,1)}, u32[]{:S(2)}) copy-start(bf16[1024,96]{0,1:T(8,128)(2,1)} %param.29) | copy-start | bytes 589828
  155.7 5.1 %collective-permute-start.3 = (f32[256,96]{0,1:T(8,128)S(1)}, f32[256,96]{0,1:T(8,128)S(1)}, u32[]{:S(2)}, u32[]{:S(2)}) collective-permute-start(f32[256,96]{0,1:T(8,128)S(1)} %fusion.74), channel_id=1, source_target_pairs={{0,32},{32,0},{64,96},{96,64},{128,160},{160,128},{192,224},{224,1... | collective-permute-start | bytes 294920 | tf_op jit(solution)/shard_map/ppermute | solution.py:25
  160.8 8.1 %collective-permute-start.4 = (f32[256,96]{0,1:T(8,128)S(1)}, f32[256,96]{0,1:T(8,128)S(1)}, u32[]{:S(2)}, u32[]{:S(2)}) collective-permute-start(f32[256,96]{0,1:T(8,128)S(1)} %add.120), channel_id=1, source_target_pairs={{0,64},{32,96},{64,0},{96,32},{128,192},{160,224},{192,128},{224,1... | collective-permute-start | bytes 294920 | tf_op jit(solution)/shard_map/ppermute | solution.py:25
  168.9 10.7 %collective-permute-start.5 = (f32[256,96]{0,1:T(8,128)S(1)}, f32[256,96]{0,1:T(8,128)S(1)}, u32[]{:S(2)}, u32[]{:S(2)}) collective-permute-start(f32[256,96]{0,1:T(8,128)S(1)} %add.121), channel_id=1, source_target_pairs={{0,128},{32,160},{64,192},{96,224},{128,0},{160,32},{192,64},{224,... | collective-permute-start | bytes 294920 | tf_op jit(solution)/shard_map/ppermute | solution.py:25
  (1 other events, 1.9 us)

commit v4 on v3

--- a/solution.py
+++ b/solution.py
@@ -40,10 +40,17 @@
     return jnp.sum(lax.all_to_all(pieces, axis, 0, 0, tiled=False).astype(sum_type), axis=0)
 
 
+def scatter_sum_flat(value, axis):
+    count = lax.axis_size(axis)
+    piece_shape = (value.shape[0] // count,) + value.shape[1:]
+    pieces = value.reshape(count, -1)
+    return jnp.sum(lax.all_to_all(pieces, axis, 0, 0, tiled=False), axis=0).reshape(piece_shape)
+
+
 def gather_rows(value, axis):
     count = lax.axis_size(axis)
-    flat = jnp.broadcast_to(value.reshape(1, -1), (count, value.size))
-    gathered = lax.all_to_all(flat, axis, 0, 0, tiled=False)
+    copies = jnp.broadcast_to(value[None], (count,) + value.shape)
+    gathered = lax.all_to_all(copies, axis, 0, 0, tiled=False)
     return gathered.reshape((count * value.shape[0],) + value.shape[1:])
 
 
@@ -123,7 +130,9 @@
     squares = jnp.sum(residual * residual, axis=1)
     normed = (residual * attn_norm).astype(jnp.bfloat16)
     partial_value = jnp.dot(normed, query_key_value_weight, preferred_element_type=jnp.float32)
-    own_value = scatter_sum(jnp.concatenate([partial_value, squares[:, None]], axis=1), "blk")
+    own_value = scatter_sum_flat(
+        jnp.concatenate([partial_value, squares[:, None]], axis=1), "blk"
+    )
     inverse = lax.rsqrt(own_value[:, -1] / MODEL_WIDTH + 1e-05)
     own_proj = (own_value[:, :-1] * inverse[:, None]).reshape(own_rows, heads_kv, col_width, HEAD_WIDTH)
     own_length = lax.dynamic_slice_in_dim(length_beam, my_index * own_rows, own_rows, 0)

time: 181 us -> 164 us (0.906)
  other arithmetic: 20.4 us -> 7.14 us
  local copies, waits for them, and re-layouts: 14 us -> 11.2 us
    broadcast_in_dim x3 -> x0, other arithmetic: 7.37 us -> none  [gather_rows(): flat = jnp.broadcast_to(value.reshape(1, -1), (count, value.size))]
    all_to_all x3 -> x0, other arithmetic: 5.44 us -> none  [gather_rows(): gathered = lax.all_to_all(flat, axis, 0, 0, tiled=False)]
    unnamed x43 -> x37, local copies, waits for them, and re-layouts: 2.7 us -> 0.57 us
    all_to_all x0 -> x1, local copies, waits for them, and re-layouts: none -> 2.04 us  [scatter_sum_flat(): lax.all_to_all(pieces, axis, 0, 0, tiled=False)]
where the time goes in v4:
time: 164 us; the launch traced here: 163 us
  waiting for transfers between devices  52.1 us (32%)
  blocking collectives  49.4 us (30%)
  starting transfers between devices  37.3 us (23%)
  local copies, waits for them, and re-layouts  11.2 us (7%)
  other arithmetic  7.14 us (4%)
  matrix products  4.72 us (3%)
    ppermute x6, waiting for transfers between devices, exchange(): return lax.ppermute(value, axis, [(i, i ^ 1 << bit) for i in range(count)])  27 us
    all_to_all x2, blocking collectives, gather_rows(): gathered = lax.all_to_all(copies, axis, 0, 0, tiled=False)  26.7 us
    all_to_all x1, blocking collectives, scatter_sum(): lax.all_to_all(pieces, axis, 0, 0, tiled=False).astype(sum_type)  22.7 us
    ppermute x6, starting transfers between devices, exchange(): return lax.ppermute(value, axis, [(i, i ^ 1 << bit) for i in range(count)])  19.5 us
    all_to_all x1, waiting for transfers between devices, scatter_sum_flat(): lax.all_to_all(pieces, axis, 0, 0, tiled=False)  9.57 us
    all_to_all x1, waiting for transfers between devices, body(): lax.all_to_all(packed, 'blk', 0, 0, tiled=False)  8.46 us
    all_to_all x1, starting transfers between devices, scatter_sum_flat(): lax.all_to_all(pieces, axis, 0, 0, tiled=False)  7.62 us
    all_to_all x1, waiting for transfers between devices, gather_rows(): gathered = lax.all_to_all(copies, axis, 0, 0, tiled=False)  7.09 us
  transfers between devices with their start and end apart: 9, of which 9 were waited for; matrix products, arithmetic and copies ran while one was open for 2% of the time, Pallas kernels for 0%

profile of v4, /device:TPU:2, one launch (start us, length us, event | category | flops | bytes accessed | tf_op | source)
XLA Modules:
  0.0 163.1 jit_solution(14732047696301059717)
XLA Ops:
  1.7 1.3 fusion.27
  3.2 2.0 %all_to_all.32 = f32[32,1,5128]{2,1,0:T(1,128)} reshape(f32[256,641]{1,0:T(8,128)S(1)} %pad_maximum_fusion) | data formatting | bytes 1312768 | tf_op jit(solution)/shard_map/all_to_all | solution.py:47
  5.2 7.6 %all-to-all-start = ((f32[32,1,5128]{2,1,0:T(1,128)}), f32[32,1,5128]{2,1,0:T(1,128)S(1)}, u32[]{:S(2)}, u32[]{:S(2)}) async-start(f32[32,1,5128]{2,1,0:T(1,128)} %all_to_all.32), calls=%async_computation | async-start | bytes 1343488 | tf_op jit(solution)/shard_map/all_to_all | solution.py:47
  15.3 9.6 %all-to-all-done = f32[32,1,5128]{2,1,0:T(1,128)S(1)} async-done(((f32[32,1,5128]{2,1,0:T(1,128)}), f32[32,1,5128]{2,1,0:T(1,128)S(1)}, u32[]{:S(2)}, u32[]{:S(2)}) %all-to-all-start) | async-done | bytes 656416 | tf_op jit(solution)/shard_map/all_to_all | solution.py:47
  26.5 5.1 %all-to-all-start.1 = ((bf16[32,8,1,3,128]{4,1,3,2,0:T(8,128)(2,1)}), bf16[32,8,1,3,128]{4,1,3,2,0:T(8,128)(2,1)S(1)}, u32[]{:S(2)}, u32[]{:S(2)}) async-start(bf16[32,8,1,3,128]{4,1,3,2,0:T(8,128)(2,1)} %broadcast_in_dim.112), calls=%async_computation.1 | async-start | bytes 393216 | tf_op jit(solution)/shard_map/all_to_all | solution.py:53
  31.6 7.1 %all-to-all-done.1 = bf16[32,8,1,3,128]{4,1,3,2,0:T(8,128)(2,1)S(1)} async-done(((bf16[32,8,1,3,128]{4,1,3,2,0:T(8,128)(2,1)}), bf16[32,8,1,3,128]{4,1,3,2,0:T(8,128)(2,1)S(1)}, u32[]{:S(2)}, u32[]{:S(2)}) %all-to-all-start.1) | async-done | bytes 196640 | tf_op jit(solution)/shard_map/all_to_all | solution.py:53
  42.0 2.1 %all_to_all.33 = f32[32,1,3120]{2,1,0:T(1,128)} reshape(f32[1,256,3,130]{3,2,1,0:T(4,128)S(1)} %copy.162) | data formatting | bytes 798720 | tf_op jit(solution)/shard_map/all_to_all | solution.py:170
  44.1 5.1 %all-to-all-start.2 = ((f32[32,1,3120]{2,1,0:T(1,128)}), f32[32,1,3120]{2,1,0:T(1,128)S(1)}, u32[]{:S(2)}, u32[]{:S(2)}) async-start(f32[32,1,3120]{2,1,0:T(1,128)} %all_to_all.33), calls=%async_computation.2 | async-start | bytes 819200 | tf_op jit(solution)/shard_map/all_to_all | solution.py:170
  50.0 8.5 %all-to-all-done.2 = f32[32,1,3120]{2,1,0:T(1,128)S(1)} async-done(((f32[32,1,3120]{2,1,0:T(1,128)}), f32[32,1,3120]{2,1,0:T(1,128)S(1)}, u32[]{:S(2)}, u32[]{:S(2)}) %all-to-all-start.2) | async-done | bytes 399392 | tf_op jit(solution)/shard_map/all_to_all | solution.py:170
  59.4 1.3 reshape.621
  63.4 11.7 %all_to_all.40 = bf16[32,8,384]{2,1,0:T(8,128)(2,1)S(1)} all-to-all(bf16[32,8,384]{2,1,0:T(8,128)(2,1)S(1)} %broadcast_in_dim.120), channel_id=1, replica_groups=mesh['kv'=8,'blk'=32] {'blk'}, dimensions={0} | all-to-all | bytes 393216 | tf_op jit(solution)/shard_map/all_to_all | solution.py:53
  75.2 2.0 %collective-permute-start = (f32[256,96]{0,1:T(8,128)S(1)}, f32[256,96]{0,1:T(8,128)S(1)}, u32[]{:S(2)}, u32[]{:S(2)}) collective-permute-start(f32[256,96]{0,1:T(8,128)S(1)} %fusion.20), channel_id=1, source_target_pairs={{0,32},{32,0},{64,96},{96,64},{128,160},{160,128},{192,224},{224,1... | collective-permute-start | bytes 294920 | tf_op jit(solution)/shard_map/ppermute | solution.py:25
  77.2 3.4 %collective-permute-done = f32[256,96]{0,1:T(8,128)S(1)} collective-permute-done((f32[256,96]{0,1:T(8,128)S(1)}, f32[256,96]{0,1:T(8,128)S(1)}, u32[]{:S(2)}, u32[]{:S(2)}) %collective-permute-start) | collective-permute-done | bytes 98336 | tf_op jit(solution)/shard_map/ppermute | solution.py:25
  80.7 3.4 %collective-permute-start.1 = (f32[256,96]{0,1:T(8,128)S(1)}, f32[256,96]{0,1:T(8,128)S(1)}, u32[]{:S(2)}, u32[]{:S(2)}) collective-permute-start(f32[256,96]{0,1:T(8,128)S(1)} %add.113), channel_id=1, source_target_pairs={{0,64},{32,96},{64,0},{96,32},{128,192},{160,224},{192,128},{224,1... | collective-permute-start | bytes 294920 | tf_op jit(solution)/shard_map/ppermute | solution.py:25
  84.0 4.9 %collective-permute-done.1 = f32[256,96]{0,1:T(8,128)S(1)} collective-permute-done((f32[256,96]{0,1:T(8,128)S(1)}, f32[256,96]{0,1:T(8,128)S(1)}, u32[]{:S(2)}, u32[]{:S(2)}) %collective-permute-start.1) | collective-permute-done | bytes 98336 | tf_op jit(solution)/shard_map/ppermute | solution.py:25
  88.9 6.4 %collective-permute-start.2 = (f32[256,96]{0,1:T(8,128)S(1)}, f32[256,96]{0,1:T(8,128)S(1)}, u32[]{:S(2)}, u32[]{:S(2)}) collective-permute-start(f32[256,96]{0,1:T(8,128)S(1)} %add.114), channel_id=1, source_target_pairs={{0,128},{32,160},{64,192},{96,224},{128,0},{160,32},{192,64},{224,... | collective-permute-start | bytes 294920 | tf_op jit(solution)/shard_map/ppermute | solution.py:25
  95.3 2.6 %collective-permute-done.2 = f32[256,96]{0,1:T(8,128)S(1)} collective-permute-done((f32[256,96]{0,1:T(8,128)S(1)}, f32[256,96]{0,1:T(8,128)S(1)}, u32[]{:S(2)}, u32[]{:S(2)}) %collective-permute-start.2) | collective-permute-done | bytes 98336 | tf_op jit(solution)/shard_map/ppermute | solution.py:25
  99.9 22.7 %all_to_all.41 = bf16[32,8,2050]{2,1,0:T(8,128)(2,1)S(1)} all-to-all(bf16[32,8,2050]{2,1,0:T(8,128)(2,1)S(1)} %concatenate.69), channel_id=1, replica_groups=mesh['kv'=8,'blk'=32] {'blk'}, dimensions={0} | all-to-all | bytes 2099200 | tf_op jit(solution)/shard_map/all_to_all | solution.py:40
  123.1 15.1 %all_to_all.42 = bf16[32,8,1024]{2,1,0:T(8,128)(2,1)S(1)} all-to-all(bf16[32,8,1024]{2,1,0:T(8,128)(2,1)S(1)} %broadcast_in_dim.121), channel_id=1, replica_groups=mesh['kv'=8,'blk'=32] {'blk'}, dimensions={0} | all-to-all | bytes 1048576 | tf_op jit(solution)/shard_map/all_to_all | solution.py:53
  138.5 5.0 %collective-permute-done.3 = f32[256,96]{0,1:T(8,128)S(1)} collective-permute-done((f32[256,96]{0,1:T(8,128)S(1)}, f32[256,96]{0,1:T(8,128)S(1)}, u32[]{:S(2)}, u32[]{:S(2)}) %collective-permute-start.3) | collective-permute-done | bytes 98336 | tf_op jit(solution)/shard_map/ppermute | solution.py:25
  143.6 3.2 %collective-permute-start.4 = (f32[256,96]{0,1:T(8,128)S(1)}, f32[256,96]{0,1:T(8,128)S(1)}, u32[]{:S(2)}, u32[]{:S(2)}) collective-permute-start(f32[256,96]{0,1:T(8,128)S(1)} %add.120), channel_id=1, source_target_pairs={{0,64},{32,96},{64,0},{96,32},{128,192},{160,224},{192,128},{224,1... | collective-permute-start | bytes 294920 | tf_op jit(solution)/shard_map/ppermute | solution.py:25
  146.8 4.8 %collective-permute-done.4 = f32[256,96]{0,1:T(8,128)S(1)} collective-permute-done((f32[256,96]{0,1:T(8,128)S(1)}, f32[256,96]{0,1:T(8,128)S(1)}, u32[]{:S(2)}, u32[]{:S(2)}) %collective-permute-start.4) | collective-permute-done | bytes 98336 | tf_op jit(solution)/shard_map/ppermute | solution.py:25
  151.7 4.5 %collective-permute-start.5 = (f32[256,96]{0,1:T(8,128)S(1)}, f32[256,96]{0,1:T(8,128)S(1)}, u32[]{:S(2)}, u32[]{:S(2)}) collective-permute-start(f32[256,96]{0,1:T(8,128)S(1)} %add.121), channel_id=1, source_target_pairs={{0,128},{32,160},{64,192},{96,224},{128,0},{160,32},{192,64},{224,... | collective-permute-start | bytes 294920 | tf_op jit(solution)/shard_map/ppermute | solution.py:25
  156.2 6.2 %collective-permute-done.5 = f32[256,96]{0,1:T(8,128)S(1)} collective-permute-done((f32[256,96]{0,1:T(8,128)S(1)}, f32[256,96]{0,1:T(8,128)S(1)}, u32[]{:S(2)}, u32[]{:S(2)}) %collective-permute-start.5) | collective-permute-done | bytes 98336 | tf_op jit(solution)/shard_map/ppermute | solution.py:25
  (118 shorter events, 16.4 us)
Async XLA Ops:
  0.6 38.0 %copy-start = (bf16[8,1,128,128]{3,2,1,0:T(8,128)(2,1)S(1)}, bf16[8,1,128,128]{3,2,1,0:T(8,128)(2,1)}, u32[]{:S(2)}) copy-start(bf16[8,1,128,128]{3,2,1,0:T(8,128)(2,1)} %param.30) | copy-start | bytes 786436
  0.6 12.2 %copy-start.11 = (s32[32]{0:T(128)S(1)}, s32[32]{0:T(128)}, u32[]{:S(2)}) copy-start(s32[32]{0:T(128)} %param.35) | copy-start | bytes 388
  0.7 12.4 %copy-start.13 = (s32[8]{0:T(128)S(1)}, s32[8]{0:T(128)}, u32[]{:S(2)}) copy-start(s32[8]{0:T(128)} %param.37) | copy-start | bytes 100
  0.7 12.4 %copy-start.14 = (s32[1,8]{1,0:T(1,128)S(1)}, s32[1,8]{1,0:T(1,128)}, u32[]{:S(2)}) copy-start(s32[1,8]{1,0:T(1,128)} %param.34) | copy-start | bytes 100
  0.7 12.4 %copy-start.4 = (bf16[8,1,127,128]{3,0,2,1:T(8,128)(2,1)S(1)}, bf16[8,1,127,128]{3,0,2,1:T(8,128)(2,1)}, u32[]{:S(2)}) copy-start(bf16[8,1,127,128]{3,0,2,1:T(8,128)(2,1)} %param.32) | copy-start | bytes 780292
  1.7 11.5 %copy-start.5 = (bf16[8,1,127,128]{3,0,2,1:T(8,128)(2,1)S(1)}, bf16[8,1,127,128]{3,0,2,1:T(8,128)(2,1)}, u32[]{:S(2)}) copy-start(bf16[8,1,127,128]{3,0,2,1:T(8,128)(2,1)} %param.33) | copy-start | bytes 780292
  3.1 10.5 %copy-start.15 = (s32[5]{0:T(128)S(1)}, s32[5]{0:T(128)}, u32[]{:S(2)}) copy-start(s32[5]{0:T(128)} %param.36) | copy-start | bytes 64
  5.2 19.7 %all-to-all-start = ((f32[32,1,5128]{2,1,0:T(1,128)}), f32[32,1,5128]{2,1,0:T(1,128)S(1)}, u32[]{:S(2)}, u32[]{:S(2)}) async-start(f32[32,1,5128]{2,1,0:T(1,128)} %all_to_all.32), calls=%async_computation | async-start | bytes 1343488 | tf_op jit(solution)/shard_map/all_to_all | solution.py:47
  26.5 12.2 %all-to-all-start.1 = ((bf16[32,8,1,3,128]{4,1,3,2,0:T(8,128)(2,1)}), bf16[32,8,1,3,128]{4,1,3,2,0:T(8,128)(2,1)S(1)}, u32[]{:S(2)}, u32[]{:S(2)}) async-start(bf16[32,8,1,3,128]{4,1,3,2,0:T(8,128)(2,1)} %broadcast_in_dim.112), calls=%async_computation.1 | async-start | bytes 393216 | tf_op jit(solution)/shard_map/all_to_all | solution.py:53
  44.1 14.4 %all-to-all-start.2 = ((f32[32,1,3120]{2,1,0:T(1,128)}), f32[32,1,3120]{2,1,0:T(1,128)S(1)}, u32[]{:S(2)}, u32[]{:S(2)}) async-start(f32[32,1,3120]{2,1,0:T(1,128)} %all_to_all.33), calls=%async_computation.2 | async-start | bytes 819200 | tf_op jit(solution)/shard_map/all_to_all | solution.py:170
  49.5 13.4 %copy-start.1 = (bf16[8,1,128,128]{3,2,0,1:T(8,128)(2,1)}, bf16[8,1,128,128]{3,2,0,1:T(8,128)(2,1)S(1)}, u32[]{:S(2)}) copy-start(bf16[8,1,128,128]{3,2,0,1:T(8,128)(2,1)S(1)} %scatter.6) | copy-start | bytes 786436
  49.7 13.4 %copy-start.3 = (bf16[8,1,128,128]{3,2,0,1:T(8,128)(2,1)}, bf16[8,1,128,128]{3,2,0,1:T(8,128)(2,1)S(1)}, u32[]{:S(2)}) copy-start(bf16[8,1,128,128]{3,2,0,1:T(8,128)(2,1)S(1)} %scatter.9) | copy-start | bytes 786436
  59.4 15.6 %copy-start.9 = (bf16[384,96]{0,1:T(8,128)(2,1)S(1)}, bf16[384,96]{0,1:T(8,128)(2,1)}, u32[]{:S(2)}) copy-start(bf16[384,96]{0,1:T(8,128)(2,1)} %param.25) | copy-start | bytes 221188
  60.8 37.1 %copy-start.2 = (bf16[1,256,96]{1,2,0:T(8,128)(2,1)S(1)}, bf16[1,256,96]{1,2,0:T(8,128)(2,1)}, u32[]{:S(2)}) copy-start(bf16[1,256,96]{1,2,0:T(8,128)(2,1)} %param.22) | copy-start | bytes 147460
  60.8 37.6 %copy-start.7 = (bf16[96,1024]{1,0:T(8,128)(2,1)S(1)}, bf16[96,1024]{1,0:T(8,128)(2,1)}, u32[]{:S(2)}) copy-start(bf16[96,1024]{1,0:T(8,128)(2,1)} %param.28) | copy-start | bytes 589828
  60.8 37.6 %copy-start.8 = (bf16[96,1024]{1,0:T(8,128)(2,1)S(1)}, bf16[96,1024]{1,0:T(8,128)(2,1)}, u32[]{:S(2)}) copy-start(bf16[96,1024]{1,0:T(8,128)(2,1)} %param.27) | copy-start | bytes 589828
  60.8 37.6 %copy-start.10 = (f32[96]{0:T(128)S(1)}, f32[96]{0:T(128)}, u32[]{:S(2)}) copy-start(f32[96]{0:T(128)} %param.26) | copy-start | bytes 1156
  75.2 5.4 %collective-permute-start = (f32[256,96]{0,1:T(8,128)S(1)}, f32[256,96]{0,1:T(8,128)S(1)}, u32[]{:S(2)}, u32[]{:S(2)}) collective-permute-start(f32[256,96]{0,1:T(8,128)S(1)} %fusion.20), channel_id=1, source_target_pairs={{0,32},{32,0},{64,96},{96,64},{128,160},{160,128},{192,224},{224,1... | collective-permute-start | bytes 294920 | tf_op jit(solution)/shard_map/ppermute | solution.py:25
  80.7 8.2 %collective-permute-start.1 = (f32[256,96]{0,1:T(8,128)S(1)}, f32[256,96]{0,1:T(8,128)S(1)}, u32[]{:S(2)}, u32[]{:S(2)}) collective-permute-start(f32[256,96]{0,1:T(8,128)S(1)} %add.113), channel_id=1, source_target_pairs={{0,64},{32,96},{64,0},{96,32},{128,192},{160,224},{192,128},{224,1... | collective-permute-start | bytes 294920 | tf_op jit(solution)/shard_map/ppermute | solution.py:25
  88.9 9.0 %collective-permute-start.2 = (f32[256,96]{0,1:T(8,128)S(1)}, f32[256,96]{0,1:T(8,128)S(1)}, u32[]{:S(2)}, u32[]{:S(2)}) collective-permute-start(f32[256,96]{0,1:T(8,128)S(1)} %add.114), channel_id=1, source_target_pairs={{0,128},{32,160},{64,192},{96,224},{128,0},{160,32},{192,64},{224,... | collective-permute-start | bytes 294920 | tf_op jit(solution)/shard_map/ppermute | solution.py:25
  99.0 39.2 %copy-start.6 = (bf16[1024,96]{0,1:T(8,128)(2,1)S(1)}, bf16[1024,96]{0,1:T(8,128)(2,1)}, u32[]{:S(2)}) copy-start(bf16[1024,96]{0,1:T(8,128)(2,1)} %param.29) | copy-start | bytes 589828
  138.4 5.1 %collective-permute-start.3 = (f32[256,96]{0,1:T(8,128)S(1)}, f32[256,96]{0,1:T(8,128)S(1)}, u32[]{:S(2)}, u32[]{:S(2)}) collective-permute-start(f32[256,96]{0,1:T(8,128)S(1)} %fusion.13), channel_id=1, source_target_pairs={{0,32},{32,0},{64,96},{96,64},{128,160},{160,128},{192,224},{224,1... | collective-permute-start | bytes 294920 | tf_op jit(solution)/shard_map/ppermute | solution.py:25
  143.6 8.1 %collective-permute-start.4 = (f32[256,96]{0,1:T(8,128)S(1)}, f32[256,96]{0,1:T(8,128)S(1)}, u32[]{:S(2)}, u32[]{:S(2)}) collective-permute-start(f32[256,96]{0,1:T(8,128)S(1)} %add.120), channel_id=1, source_target_pairs={{0,64},{32,96},{64,0},{96,32},{128,192},{160,224},{192,128},{224,1... | collective-permute-start | bytes 294920 | tf_op jit(solution)/shard_map/ppermute | solution.py:25
  151.7 10.7 %collective-permute-start.5 = (f32[256,96]{0,1:T(8,128)S(1)}, f32[256,96]{0,1:T(8,128)S(1)}, u32[]{:S(2)}, u32[]{:S(2)}) collective-permute-start(f32[256,96]{0,1:T(8,128)S(1)} %add.121), channel_id=1, source_target_pairs={{0,128},{32,160},{64,192},{96,224},{128,0},{160,32},{192,64},{224,... | collective-permute-start | bytes 294920 | tf_op jit(solution)/shard_map/ppermute | solution.py:25
  (1 other events, 1.9 us)
